TPU v7x, 512 devices: a whole 4x4x16 slice. The times are simulated.
512 devices in a mesh: req: 16 (over z), tp: 32 (over x, y, core).
Axes of the slice: x: 4, y: 4, z: 16, core: 2. Of those that a mesh axis runs over, the one named last changes fastest.
Arguments:
- hidden: bfloat16 [1024, 5120], P(('req', 'tp')), may hold values from -6 to 6
- input_norm_gain: float32 [5120], replicated, may hold values from 0.1 to 1.9
- query_weight: bfloat16 [5120, 4096], P(None, 'tp'), may hold values from -1 to 1
- key_weight: bfloat16 [128, 8, 5120], P('tp'), may hold values from -0.078125 to 0.078125
- value_weight: bfloat16 [128, 8, 5120], P('tp'), may hold values from -0.078125 to 0.078125
- output_weight: bfloat16 [4096, 5120], P('tp'), may hold values from -0.09375 to 0.09375
- query_bias_vector: float32 [4096], P('tp'), may hold values from -3 to 3
- value_bias_vector: float32 [128, 8], P('tp'), may hold values from -3 to 3
- adapter_down_maps: bfloat16 [16, 5120, 32], P('req', 'tp'), may hold values from -0.078125 to 0.078125
- adapter_query_up: bfloat16 [16, 16, 4096], P('req', None, 'tp'), may hold values from -1.5 to 1.5
- adapter_value_up: bfloat16 [16, 16, 128, 8], P('req', None, 'tp'), may hold values from -1.5 to 1.5
- lengths: int32 [16, 8], P('req'), may hold values from 1 to 32, 64 in all within a row
- prompt_adapter: int32 [16, 8], P('req'), may hold values from 0 to 15
Outputs:
- output: bfloat16 [1024, 5120], P(('req', 'tp'))
All inputs are finite; a program needn't handle non-finite values.
Results may differ from a plain program's by a relative error of at most 0.019.
Values may be sent and summed in bfloat16 or wider, within the bound.
No kernel may reach another device: no remote copies, remote signals or barrier semaphores. Data moves between devices by JAX's collectives and lax.ppermute only.
A program may use at most 128 MiB of HBM per device.

v0:
```python
import jax
import jax.numpy as jnp
from jax import lax
from jax.sharding import PartitionSpec as P

HD = 128
HK = 8
HQ = 32


eps = 1e-06
rope_base = 1000000.0


def prompt_layout(prompt_length_list, group_tokens):
    ends = jnp.cumsum(prompt_length_list)
    starts = ends - prompt_length_list
    places = jnp.arange(group_tokens, dtype=jnp.int32)
    group_entry = (places[:, None] >= starts[None, :]) & (places[:, None] < ends[None, :])
    chosen = group_entry.astype(jnp.int32)
    segment = jnp.sum(
        chosen * jnp.arange(prompt_length_list.shape[0], dtype=jnp.int32)[None, :], axis=1
    )
    offset = places - jnp.sum(chosen * starts[None, :], axis=1)
    return (group_entry, segment, offset)


def rms_rows(source, input_norm_gain):
    values = source.astype(jnp.float32)
    return (
        values
        * lax.rsqrt(jnp.mean(values * values, axis=-1, keepdims=True) + eps)
        * input_norm_gain
    ).astype(jnp.bfloat16)


def rotate(values, offset):
    width = values.shape[-1]
    half_width = width // 2
    frequency = rope_base ** (-(jnp.arange(half_width, dtype=jnp.float32) * 2.0) / width)
    angles = offset.astype(jnp.float32)[:, None] * frequency[None, :]
    cosine = jnp.cos(angles)[:, None, :]
    sines = jnp.sin(angles)[:, None, :]
    lower_half = values[..., :half_width]
    upper_half = values[..., half_width:]
    return jnp.concatenate(
        [lower_half * cosine - upper_half * sines, upper_half * cosine + lower_half * sines],
        axis=-1,
    )


def select_table(table, adapter_choice_list):
    chosen = (
        adapter_choice_list[:, None] == jnp.arange(table.shape[0], dtype=jnp.int32)[None, :]
    ).astype(jnp.bfloat16)
    flat = jnp.dot(chosen, table.reshape(table.shape[0], -1), preferred_element_type=jnp.float32)
    return flat.astype(jnp.bfloat16).reshape((adapter_choice_list.shape[0],) + table.shape[1:])


def rank_terms(normed_rows, group_entry, down_table):
    terms = jnp.einsum("td,sdr->tsr", normed_rows, down_table, preferred_element_type=jnp.float32)
    return jnp.sum(jnp.where(group_entry[:, :, None], terms, jnp.float32(0.0)), axis=1)


def reduced_rank_term(hidden_code, group_entry, table):
    row_count = hidden_code.shape[0]
    spread = jnp.where(
        group_entry[:, :, None], hidden_code[:, None, :], jnp.zeros((), jnp.bfloat16)
    )
    return jnp.dot(
        spread.reshape(row_count, -1),
        table.reshape(-1, table.shape[-1]),
        preferred_element_type=jnp.float32,
    )


def attend(query_rot, key_rot, value_head, segment):
    scores = jnp.einsum(
        "qhd,kd->hqk", query_rot, key_rot, preferred_element_type=jnp.float32
    ) * HD ** (-0.5)
    places = jnp.arange(segment.shape[0], dtype=jnp.int32)
    allowed = (segment[:, None] == segment[None, :]) & (places[None, :] <= places[:, None])
    scores = jnp.where(allowed[None], scores, jnp.float32(-1e30))
    row_max = jnp.max(scores, axis=-1, keepdims=True)
    weights = jnp.exp(scores - row_max)
    probabilities = (weights / jnp.sum(weights, axis=-1, keepdims=True)).astype(jnp.bfloat16)
    mixed = jnp.einsum("hqk,kd->qhd", probabilities, value_head, preferred_element_type=jnp.float32)
    return mixed.astype(jnp.bfloat16)


def shards(
    hidden,
    input_norm_gain,
    query_weight,
    key_weight,
    value_weight,
    output_weight,
    query_bias_vector,
    value_bias_vector,
    adapter_down_maps,
    adapter_query_up,
    adapter_value_up,
    lengths,
    prompt_adapter,
):
    tp_width = lax.axis_size("tp")
    tp_place = lax.axis_index("tp")
    tok_rows = hidden.shape[0]
    group_tokens = tok_rows * tp_width
    rank_extent = adapter_query_up.shape[1]
    entry_slice = key_weight.shape[0]
    kv_heads = key_weight.shape[1]
    bank_down, bank_query, bank_value = (
        lax.all_gather(adapter_down_maps, "req", axis=0, tiled=True),
        lax.all_gather(adapter_query_up, "req", axis=0, tiled=True),
        lax.all_gather(adapter_value_up, "req", axis=0, tiled=True),
    )
    prompt_length_list = lengths[0]
    adapter_choice_list = prompt_adapter[0]
    group_entry, segment, offset = prompt_layout(prompt_length_list, group_tokens)
    full_down = lax.all_gather(bank_down, "tp", axis=1, tiled=True)
    own_normed = rms_rows(hidden, input_norm_gain)
    own_member = lax.dynamic_slice_in_dim(group_entry, tp_place * tok_rows, tok_rows, 0)
    own_latent = rank_terms(
        own_normed, own_member, select_table(full_down, adapter_choice_list)
    ).astype(jnp.bfloat16)
    gathered, hidden_code = (
        lax.all_gather(hidden, "tp", axis=0, tiled=True),
        lax.all_gather(own_latent, "tp", axis=0, tiled=True),
    )
    normalized_input = rms_rows(gathered, input_norm_gain)
    query_rows = (
        jnp.dot(normalized_input, query_weight, preferred_element_type=jnp.float32)
        + query_bias_vector
    )
    query_rows = query_rows + reduced_rank_term(
        hidden_code[:, :rank_extent], group_entry, select_table(bank_query, adapter_choice_list)
    )
    key_cols = jnp.einsum(
        "tm,ehm->teh", normalized_input, key_weight, preferred_element_type=jnp.float32
    ).astype(jnp.bfloat16)
    value_cols = (
        jnp.einsum(
            "tm,ehm->teh", normalized_input, value_weight, preferred_element_type=jnp.float32
        )
        + value_bias_vector[None, :, :]
    )
    value_table = select_table(bank_value, adapter_choice_list)
    value_table = value_table.reshape(
        value_table.shape[0], value_table.shape[1], entry_slice * kv_heads
    )
    value_extra = reduced_rank_term(hidden_code[:, rank_extent:], group_entry, value_table).reshape(
        group_tokens, entry_slice, kv_heads
    )
    value_cols = (value_cols + value_extra).astype(jnp.bfloat16)
    key_all, value_all = (
        lax.all_gather(key_cols, "tp", axis=1, tiled=True),
        lax.all_gather(value_cols, "tp", axis=1, tiled=True),
    )
    head_count = query_weight.shape[1] // HD
    kv_index = tp_place * head_count // (HQ // HK)
    key_head = lax.dynamic_slice_in_dim(key_all, kv_index, 1, 2)[:, :, 0]
    value_head = lax.dynamic_slice_in_dim(value_all, kv_index, 1, 2)[:, :, 0]
    key_rot = rotate(key_head.astype(jnp.float32).reshape(group_tokens, 1, HD), offset)[
        :, 0, :
    ].astype(jnp.bfloat16)
    query_rot = rotate(query_rows.reshape(group_tokens, head_count, HD), offset).astype(
        jnp.bfloat16
    )
    mixed_heads = attend(query_rot, key_rot, value_head, segment).reshape(
        group_tokens, head_count * HD
    )
    projected = lax.psum_scatter(
        jnp.dot(mixed_heads, output_weight, preferred_element_type=jnp.float32).astype(
            jnp.bfloat16
        ),
        "tp",
        scatter_dimension=0,
        tiled=True,
    ).astype(jnp.float32)
    return (hidden.astype(jnp.float32) + projected).astype(jnp.bfloat16)


def solution(mesh):
    return jax.shard_map(
        shards,
        mesh=mesh,
        in_specs=(
            P(("req", "tp"), None),
            P(),
            P(None, "tp"),
            P("tp", None, None),
            P("tp", None, None),
            P("tp", None),
            P("tp"),
            P("tp", None),
            P("req", "tp", None),
            P("req", None, "tp"),
            P("req", None, "tp", None),
            P("req", None),
            P("req", None),
        ),
        out_specs=P(("req", "tp"), None),
        check_vma=False,
    )
```

profile of v0, /device:TPU:1, one launch (start us, length us, event | category | flops | bytes accessed | tf_op | source)
XLA Modules:
  0.0 415.1 jit_solution(5436439434987863532)
XLA Ops:
  6.5 0.0 copy-start
  6.5 0.0 all-gather.4.cloned.1.call-start
  6.5 30.8 %all_gather.25 = bf16[16,160,32]{1,2,0:T(8,128)(2,1)S(1)} all-gather(bf16[1,160,32]{1,2,0:T(8,128)(2,1)} %param.21), channel_id=1, replica_groups=mesh['req'=16,'tp'=32] {'req'}, dimensions={0}, use_global_device_ids=true | all-gather | bytes 174080 | tf_op jit(solution)/shard_map/all_gather | solution.py:114
  37.4 1.3 copy.39
  38.7 0.0 all-gather.4.cloned.1.call-update
  38.7 0.0 all-reduce.3.cloned.1.call-start
  38.8 0.0 copy-done.11
  38.8 0.2 reduce-window.4
  39.0 0.0 copy-done.2
  39.0 33.7 %all-gather = bf16[32,2,5120]{2,1,0:T(2,128)(2,1)S(1)} all-gather(bf16[1,2,5120]{2,1,0:T(2,128)(2,1)S(1)} %bitcast.83), channel_id=1, replica_groups=mesh['req'=16,'tp'=32] {'tp'}, dimensions={0}, use_global_device_ids=true | all-gather | bytes 675840 | tf_op jit(solution)/shard_map/all_gather | solution.py:128
  72.6 0.2 reshape.336
  72.8 0.0 copy-done.6
  72.8 0.0 copy-start.5
  72.8 20.4 %all_gather.28 = bf16[16,16,4,8]{1,3,2,0:T(8,128)(2,1)S(1)} all-gather(bf16[1,16,4,8]{1,3,2,0:T(8,128)(2,1)S(1)} %copy-done.6), channel_id=1, replica_groups=mesh['req'=16,'tp'=32] {'req'}, dimensions={0}, use_global_device_ids=true | all-gather | bytes 17408 | tf_op jit(solution)/shard_map/all_gather | solution.py:116
  93.2 0.3 copy.43
  93.5 0.0 copy-done.9
  93.6 0.2 convolution_convert_fusion.5
  93.7 0.1 reshape_reshape_reshape.3
  93.8 0.1 copy.44
  93.9 0.0 copy-done.7
  93.9 23.8 %all_gather.31 = bf16[16,16,128]{2,1,0:T(8,128)(2,1)S(1)} all-gather(bf16[1,16,128]{2,1,0:T(8,128)(2,1)S(1)} %copy-done.7), channel_id=1, replica_groups=mesh['req'=16,'tp'=32] {'req'}, dimensions={0}, use_global_device_ids=true | all-gather | bytes 69632 | tf_op jit(solution)/shard_map/all_gather | solution.py:115
  117.7 0.2 convolution_convert_fusion.2
  117.9 0.2 multiply_reduce_fusion
  118.1 0.0 copy-done.5
  118.2 0.0 copy-start.4
  118.2 0.0 copy-start.8
  118.2 0.2 multiply_convert_fusion
  118.4 0.7 copy-done.3
  119.1 0.3 convolution_convert_fusion.4
  119.4 34.9 %all_gather.30 = bf16[64,128,8]{0,2,1:T(8,128)(2,1)S(1)} all-gather(bf16[64,4,8]{0,2,1:T(8,128)(2,1)S(1)} %convolution_convert_fusion.4), channel_id=1, replica_groups=mesh['req'=16,'tp'=32] {'tp'}, dimensions={1}, use_global_device_ids=true | all-gather | bytes 135168 | tf_op jit(solution)/shard_map/all_gather | solution.py:157
  154.3 0.1 fusion.48
  154.4 0.1 constant_dynamic-slice_fusion.2
  154.5 0.1 select_reduce_fusion.1
  154.6 0.2 fusion.18
  154.7 0.0 copy-done.4
  154.8 0.0 copy-done.8
  154.8 0.3 convolution_add_fusion.3
  155.1 0.0 copy-done.1
  155.1 0.0 copy-done.10
  155.1 0.4 convolution_add_fusion.1
  155.5 0.0 all-gather.4.cloned.1.call-done
  155.5 19.0 %copy.40 = bf16[16,5120,32]{2,1,0:T(8,128)(2,1)} copy(bf16[16,5120,32]{2,0,1:T(8,128)(2,1)} %all-gather.4.cloned.1.call-done) | data formatting | bytes 10485760 | tf_op jit(solution)/shard_map/all_gather | solution.py:121
  174.5 33.3 %reshape.324 = bf16[16,163840]{1,0:T(8,128)(2,1)} reshape(bf16[16,5120,32]{2,1,0:T(8,128)(2,1)} %copy.40) | data formatting | bytes 10485760 | tf_op jit(solution)/shard_map/reshape | solution.py:56
  207.7 4.9 %convolution_convert_fusion = bf16[8,163840]{1,0:T(8,128)(2,1)} fusion(bf16[16,163840]{1,0:T(8,128)(2,1)} %reshape.324, s32[8]{0:T(128)S(1)} %bitcast.92), kind=kOutput, calls=%fused_computation | convolution fusion | flops 43253888 | bytes 7864352 | tf_op jit(solution)/shard_map/dot_general | solution.py:56
  212.6 4.4 %reshape.341 = bf16[1310720]{0:T(1024)(128)(2,1)} reshape(bf16[8,163840]{1,0:T(8,128)(2,1)} %convolution_convert_fusion) | data formatting | bytes 5242880
  217.0 12.1 %reshape.325 = bf16[8,5120,32]{2,1,0:T(8,128)(2,1)} reshape(bf16[1310720]{0:T(1024)(128)(2,1)} %reshape.341) | data formatting | bytes 5242880 | tf_op jit(solution)/shard_map/reshape | solution.py:57
  229.2 5.5 %fusion.5 = bf16[2,32]{1,0:T(2,128)(2,1)S(1)} fusion(bf16[8,5120,32]{2,1,0:T(8,128)(2,1)} %reshape.325, bf16[2,5120]{1,0:T(2,128)(2,1)S(1)} %copy-done.2, f32[2]{0:T(128)S(1)} %add_rsqrt_fusion, f32[5120]{0:T(1024)S(1)} %copy-done.5, pred[2,8]{0,1:T(8,128)(4,1)S(1)} %constant_dynamic-slice_fusion.2), kind=kOutput, calls=%fused_computation.19 | convolution fusion | flops 5284800 | bytes 2662552 | tf_op jit(solution)/shard_map/td,sdr->tsr/dot_general | solution.py:61
  234.6 19.1 %all-gather.1 = bf16[32,2,32]{2,1,0:T(2,128)(2,1)S(1)} all-gather(bf16[1,2,32]{2,1,0:T(2,128)(2,1)S(1)} %bitcast.93), channel_id=1, replica_groups=mesh['req'=16,'tp'=32] {'tp'}, dimensions={0}, use_global_device_ids=true | all-gather | bytes 4224 | tf_op jit(solution)/shard_map/all_gather | solution.py:129
  253.7 0.1 fusion.54
  253.8 0.1 copy.42
  253.9 0.1 copy.48
  254.0 0.1 fusion.4
  254.1 23.6 %all_gather.29 = bf16[64,128,8]{0,2,1:T(8,128)(2,1)S(1)} all-gather(bf16[64,4,8]{0,2,1:T(8,128)(2,1)S(1)} %fusion.4), channel_id=1, replica_groups=mesh['req'=16,'tp'=32] {'tp'}, dimensions={1}, use_global_device_ids=true | all-gather | bytes 135168 | tf_op jit(solution)/shard_map/all_gather | solution.py:158
  277.8 0.1 constant_dynamic-slice_fusion
  277.9 0.1 copy.53
  278.0 0.1 copy.52
  278.1 0.2 fusion.1
  278.3 0.2 fusion.46
  278.5 0.2 fusion.55
  278.8 1.4 convolution_convert_fusion.1
  280.2 0.0 all-reduce.3.cloned.1.call-update
  280.2 1.3 dynamic-slice
  282.1 124.7 %all-reduce.3.cloned.1.call-done = bf16[64,5120]{1,0:T(8,128)(2,1)} async-done(((bf16[64,5120]{1,0:T(8,128)(2,1)}), bf16[64,5120]{1,0:T(8,128)(2,1)}) %all-reduce.3.cloned.1.call-update) | async-done | bytes 655376
  406.8 1.5 fusion.21
  (18 shorter events, 0.1 us)
Async XLA Ops:
  6.5 272.2 %copy-start = (bf16[128,5120]{1,0:T(8,128)(2,1)S(1)}, bf16[128,5120]{1,0:T(8,128)(2,1)}, u32[]{:S(2)}) copy-start(bf16[128,5120]{1,0:T(8,128)(2,1)} %param.18) | copy-start | bytes 3932164
  6.5 32.2 %copy-start.11 = (s32[1,8]{1,0:T(1,128)S(1)}, s32[1,8]{1,0:T(1,128)}, u32[]{:S(2)}) copy-start(s32[1,8]{1,0:T(1,128)} %param.24) | copy-start | bytes 100
  6.5 32.4 %copy-start.2 = (bf16[2,5120]{1,0:T(2,128)(2,1)S(1)}, bf16[2,5120]{1,0:T(2,128)(2,1)}, u32[]{:S(2)}) copy-start(bf16[2,5120]{1,0:T(2,128)(2,1)} %param.13) | copy-start | bytes 61444
  6.5 148.9 %all-gather.4.cloned.1.call-start = ((), (), s32[]{:S(2)}) async-start(), calls=%async_computation | async-start | bytes 21626880 | tf_op jit(solution)/shard_map/all_gather | solution.py:121
  38.7 368.1 %all-reduce.3.cloned.1.call-start = ((), (), s32[]{:S(2)}) async-start(), calls=%async_computation.1 | async-start | bytes 1310720
  39.0 33.8 %copy-start.6 = (bf16[1,16,4,8]{1,3,2,0:T(8,128)(2,1)S(1)}, bf16[1,16,4,8]{1,3,2,0:T(8,128)(2,1)}, u32[]{:S(2)}) copy-start(bf16[1,16,4,8]{1,3,2,0:T(8,128)(2,1)} %param.23) | copy-start | bytes 3076
  72.6 20.9 %copy-start.9 = (s32[1,8]{1,0:T(1,128)S(1)}, s32[1,8]{1,0:T(1,128)}, u32[]{:S(2)}) copy-start(s32[1,8]{1,0:T(1,128)} %param.25) | copy-start | bytes 100
  72.6 21.3 %copy-start.7 = (bf16[1,16,128]{2,1,0:T(8,128)(2,1)S(1)}, bf16[1,16,128]{2,1,0:T(8,128)(2,1)}, u32[]{:S(2)}) copy-start(bf16[1,16,128]{2,1,0:T(8,128)(2,1)} %param.22) | copy-start | bytes 12292
  72.8 45.3 %copy-start.5 = (f32[5120]{0:T(1024)S(1)}, f32[5120]{0:T(1024)}, u32[]{:S(2)}) copy-start(f32[5120]{0:T(1024)} %param.14) | copy-start | bytes 61444
  118.1 1.0 copy-start.3
  118.2 36.6 %copy-start.4 = (bf16[4,8,5120]{2,1,0:T(8,128)(2,1)S(1)}, bf16[4,8,5120]{2,1,0:T(8,128)(2,1)}, u32[]{:S(2)}) copy-start(bf16[4,8,5120]{2,1,0:T(8,128)(2,1)} %param.17) | copy-start | bytes 983044
  118.2 36.6 %copy-start.8 = (f32[4,8]{1,0:T(4,128)S(1)}, f32[4,8]{1,0:T(4,128)}, u32[]{:S(2)}) copy-start(f32[4,8]{1,0:T(4,128)} %param.20) | copy-start | bytes 388
  119.1 35.9 %copy-start.1 = (bf16[5120,128]{1,0:T(8,128)(2,1)S(1)}, bf16[5120,128]{1,0:T(8,128)(2,1)}, u32[]{:S(2)}) copy-start(bf16[5120,128]{1,0:T(8,128)(2,1)} %param.15) | copy-start | bytes 3932164
  119.1 36.0 %copy-start.10 = (f32[128]{0:T(128)S(1)}, f32[128]{0:T(128)}, u32[]{:S(2)}) copy-start(f32[128]{0:T(128)} %param.19) | copy-start | bytes 1540
Sparse Core Ops, SparseCore 0:
  38.8 101.3 all-gather.3
  280.3 126.4 all-reduce.2
where the time goes:
time: 416 us; the launch traced here: 415 us
  blocking collectives  186 us (45%)
  waiting for transfers between devices  125 us (30%)
  local copies, waits for them, and re-layouts  73.5 us (18%)
  between operations  14.3 us (3%)
  matrix products  13.6 us (3%)
    unnamed x3, waiting for transfers between devices  125 us
    all_gather x1, blocking collectives, shards(): lax.all_gather(key_cols, 'tp', axis=1, tiled=True)  34.9 us
    all_gather x1, blocking collectives, shards(): lax.all_gather(hidden, 'tp', axis=0, tiled=True)  33.7 us
    reshape x1, local copies, waits for them, and re-layouts, select_table(): table.reshape(table.shape[0], -1)  33.3 us
    all_gather x1, blocking collectives, shards(): lax.all_gather(adapter_down_maps, 'req', axis=0, tiled=True)  30.8 us
    all_gather x1, blocking collectives, shards(): lax.all_gather(adapter_query_up, 'req', axis=0, tiled=True)  23.8 us
    all_gather x1, blocking collectives, shards(): lax.all_gather(value_cols, 'tp', axis=1, tiled=True)  23.6 us
    all_gather x1, blocking collectives, shards(): lax.all_gather(adapter_value_up, 'req', axis=0, tiled=True)  20.4 us
  transfers between devices with their start and end apart: 2, of which 1 were waited for; matrix products, arithmetic and copies ran while one was open for 1% of the time, Pallas kernels for 0%

commit v1 on v0

v1 whole, which is shorter than its diff:
```python
import jax
import jax.numpy as jnp
from jax import lax
from jax.sharding import PartitionSpec as P

HD = 128
HK = 8
HQ = 32


eps = 1e-06
rope_base = 1000000.0


def prompt_layout(prompt_length_list, group_tokens):
    ends = jnp.cumsum(prompt_length_list)
    starts = ends - prompt_length_list
    places = jnp.arange(group_tokens, dtype=jnp.int32)
    group_entry = (places[:, None] >= starts[None, :]) & (places[:, None] < ends[None, :])
    chosen = group_entry.astype(jnp.int32)
    segment = jnp.sum(
        chosen * jnp.arange(prompt_length_list.shape[0], dtype=jnp.int32)[None, :], axis=1
    )
    offset = places - jnp.sum(chosen * starts[None, :], axis=1)
    return (group_entry, segment, offset)


def rms_rows(source, input_norm_gain):
    values = source.astype(jnp.float32)
    return (
        values
        * lax.rsqrt(jnp.mean(values * values, axis=-1, keepdims=True) + eps)
        * input_norm_gain
    ).astype(jnp.bfloat16)


def rotate(values, offset):
    width = values.shape[-1]
    half_width = width // 2
    frequency = rope_base ** (-(jnp.arange(half_width, dtype=jnp.float32) * 2.0) / width)
    angles = offset.astype(jnp.float32)[:, None] * frequency[None, :]
    cosine = jnp.cos(angles)[:, None, :]
    sines = jnp.sin(angles)[:, None, :]
    lower_half = values[..., :half_width]
    upper_half = values[..., half_width:]
    return jnp.concatenate(
        [lower_half * cosine - upper_half * sines, upper_half * cosine + lower_half * sines],
        axis=-1,
    )


def attend(query_rot, key_rot, value_head, segment):
    scores = jnp.einsum(
        "qhd,kd->hqk", query_rot, key_rot, preferred_element_type=jnp.float32
    ) * HD ** (-0.5)
    places = jnp.arange(segment.shape[0], dtype=jnp.int32)
    allowed = (segment[:, None] == segment[None, :]) & (places[None, :] <= places[:, None])
    scores = jnp.where(allowed[None], scores, jnp.float32(-1e30))
    row_max = jnp.max(scores, axis=-1, keepdims=True)
    weights = jnp.exp(scores - row_max)
    probabilities = (weights / jnp.sum(weights, axis=-1, keepdims=True)).astype(jnp.bfloat16)
    mixed = jnp.einsum("hqk,kd->qhd", probabilities, value_head, preferred_element_type=jnp.float32)
    return mixed.astype(jnp.bfloat16)


def shards(
    hidden,
    input_norm_gain,
    query_weight,
    key_weight,
    value_weight,
    output_weight,
    query_bias_vector,
    value_bias_vector,
    adapter_down_maps,
    adapter_query_up,
    adapter_value_up,
    lengths,
    prompt_adapter,
):
    tp_width = lax.axis_size("tp")
    tp_place = lax.axis_index("tp")
    tok_rows = hidden.shape[0]
    group_tokens = tok_rows * tp_width
    rank_extent = adapter_query_up.shape[1]
    entry_slice = key_weight.shape[0]
    kv_heads = key_weight.shape[1]
    feat_slice = adapter_down_maps.shape[1]
    head_count = query_weight.shape[1] // HD

    down_flat = adapter_down_maps.reshape(1, -1)
    query_flat = adapter_query_up.reshape(1, -1)
    value_flat = adapter_value_up.reshape(1, -1)
    bank = lax.all_gather(
        jnp.concatenate([down_flat, query_flat, value_flat], axis=1), "req", axis=0, tiled=True
    )
    adapter_total = bank.shape[0]
    n_down, n_query = down_flat.shape[1], query_flat.shape[1]
    bank_down = bank[:, :n_down].reshape((adapter_total,) + adapter_down_maps.shape[1:])
    bank_query = bank[:, n_down : n_down + n_query].reshape(
        (adapter_total,) + adapter_query_up.shape[1:]
    )
    bank_value = bank[:, n_down + n_query :].reshape((adapter_total,) + adapter_value_up.shape[1:])

    prompt_length_list = lengths[0]
    adapter_choice_list = prompt_adapter[0]
    group_entry, segment, offset = prompt_layout(prompt_length_list, group_tokens)
    token_adapter = jnp.take(adapter_choice_list, segment)
    adapter_pick = token_adapter[:, None] == jnp.arange(adapter_total, dtype=jnp.int32)[None, :]

    gathered = lax.all_gather(hidden, "tp", axis=0, tiled=True)
    normalized_input = rms_rows(gathered, input_norm_gain)

    own_features = lax.dynamic_slice_in_dim(
        normalized_input, tp_place * feat_slice, feat_slice, 1
    )
    terms = jnp.einsum(
        "tf,afr->tar", own_features, bank_down, preferred_element_type=jnp.float32
    )
    latent_part = jnp.sum(jnp.where(adapter_pick[:, :, None], terms, 0.0), axis=1)

    key_cols = jnp.einsum(
        "tm,ehm->the", normalized_input, key_weight, preferred_element_type=jnp.float32
    )
    value_cols = (
        jnp.einsum(
            "tm,ehm->the", normalized_input, value_weight, preferred_element_type=jnp.float32
        )
        + jnp.transpose(value_bias_vector)[None, :, :]
    )
    dest = jnp.arange(tp_width, dtype=jnp.int32)
    dest_head = dest * head_count // (HQ // HK)
    key_send = jnp.take(key_cols, dest_head, axis=1).transpose(1, 0, 2).reshape(tp_width, -1)
    value_send = jnp.take(value_cols, dest_head, axis=1).transpose(1, 0, 2).reshape(tp_width, -1)
    latent_send = jnp.broadcast_to(latent_part.reshape(1, -1), (tp_width, latent_part.size))
    up_send = (
        jnp.take(bank_value, dest_head, axis=3)
        .astype(jnp.float32)
        .transpose(3, 0, 1, 2)
        .reshape(tp_width, -1)
    )
    n_key, n_value, n_latent = key_send.shape[1], value_send.shape[1], latent_send.shape[1]
    received = lax.all_to_all(
        jnp.concatenate([key_send, value_send, latent_send, up_send], axis=1),
        "tp",
        0,
        0,
        tiled=True,
    )
    key_head = (
        received[:, :n_key]
        .reshape(tp_width, group_tokens, entry_slice)
        .transpose(1, 0, 2)
        .reshape(group_tokens, HD)
        .astype(jnp.bfloat16)
    )
    value_base = (
        received[:, n_key : n_key + n_value]
        .reshape(tp_width, group_tokens, entry_slice)
        .transpose(1, 0, 2)
        .reshape(group_tokens, HD)
    )
    latent = (
        jnp.sum(
            received[:, n_key + n_value : n_key + n_value + n_latent].reshape(
                tp_width, group_tokens, 2 * rank_extent
            ),
            axis=0,
        )
        .astype(jnp.bfloat16)
    )
    value_up_head = (
        received[:, n_key + n_value + n_latent :]
        .reshape(tp_width, adapter_total, rank_extent, entry_slice)
        .transpose(1, 2, 0, 3)
        .reshape(adapter_total, rank_extent, HD)
    )

    pick = adapter_pick.astype(jnp.bfloat16)
    query_latent = (latent[:, None, :rank_extent] * pick[:, :, None]).reshape(group_tokens, -1)
    value_latent = (latent[:, None, rank_extent:] * pick[:, :, None]).reshape(group_tokens, -1)
    query_rows = (
        jnp.dot(normalized_input, query_weight, preferred_element_type=jnp.float32)
        + query_bias_vector
        + jnp.dot(
            query_latent,
            bank_query.reshape(-1, bank_query.shape[-1]),
            preferred_element_type=jnp.float32,
        )
    )
    value_head = (
        value_base
        + jnp.dot(
            value_latent,
            value_up_head.astype(jnp.bfloat16).reshape(-1, HD),
            preferred_element_type=jnp.float32,
        )
    ).astype(jnp.bfloat16)

    key_rot = rotate(key_head.astype(jnp.float32).reshape(group_tokens, 1, HD), offset)[
        :, 0, :
    ].astype(jnp.bfloat16)
    query_rot = rotate(query_rows.reshape(group_tokens, head_count, HD), offset).astype(
        jnp.bfloat16
    )
    mixed_heads = attend(query_rot, key_rot, value_head, segment).reshape(
        group_tokens, head_count * HD
    )
    block_terms = jnp.dot(mixed_heads, output_weight, preferred_element_type=jnp.float32).astype(
        jnp.bfloat16
    )
    owner_terms = lax.all_to_all(
        block_terms.reshape(tp_width, tok_rows, block_terms.shape[-1]), "tp", 0, 0, tiled=True
    )
    projected = jnp.sum(owner_terms.astype(jnp.float32), axis=0)
    return (hidden.astype(jnp.float32) + projected).astype(jnp.bfloat16)


def solution(mesh):
    return jax.shard_map(
        shards,
        mesh=mesh,
        in_specs=(
            P(("req", "tp"), None),
            P(),
            P(None, "tp"),
            P("tp", None, None),
            P("tp", None, None),
            P("tp", None),
            P("tp"),
            P("tp", None),
            P("req", "tp", None),
            P("req", None, "tp"),
            P("req", None, "tp", None),
            P("req", None),
            P("req", None),
        ),
        out_specs=P(("req", "tp"), None),
        check_vma=False,
    )
```

time: 416 us -> 125 us (0.30)
  waiting for transfers between devices: 125 us -> 9.73 us
  blocking collectives: 186 us -> 81.2 us
  local copies, waits for them, and re-layouts: 73.5 us -> 15.1 us
  between operations: 14.3 us -> 0.53 us
  matrix products: 13.6 us -> 3.47 us
  other arithmetic: 2.75 us -> 9.57 us
  starting transfers between devices: 0.04 us -> 5.1 us
    unnamed x3 -> x0, waiting for transfers between devices: 125 us -> none
    all_gather x7 -> x2, blocking collectives: 186 us -> 64.9 us  [the longest x1 33.2 us: shards(): gathered = lax.all_gather(hidden, 'tp', axis=0, tiled=True)]
    reshape x2 -> x11, local copies, waits for them, and re-layouts: 45.4 us -> 2.64 us  [the longest x2 1.03 us: shards(): up_send = jnp.take(bank_value, dest_head, axis=3).astype(jnp.float32).tra...]
    all_gather x3 -> x0, local copies, waits for them, and re-layouts: 20.6 us -> none  [the longest x1 19 us: shards(): full_down = lax.all_gather(bank_down, 'tp', axis=1, tiled=True)]
    all_to_all x0 -> x1, blocking collectives: none -> 16.3 us  [shards(): lax.all_to_all(block_terms.reshape(tp_width, tok_rows, block_terms.shape[...]
    all_to_all x0 -> x1, waiting for transfers between devices: none -> 9.73 us  [shards(): lax.all_to_all(jnp.concatenate([key_send, value_send, latent_send, up_sen...]
    dot_general x8 -> x4, matrix products: 11.6 us -> 2.09 us  [the longest x1 1.28 us: shards(): jnp.einsum('tm,ehm->the', normalized_input, value_weight, preferred_eleme...]
    select_n x1 -> x4, other arithmetic: 0.03 us -> 5.58 us  [the longest x1 5.47 us: shards(): token_adapter = jnp.take(adapter_choice_list, segment)]
  transfers between devices with their start and end apart: 2 -> 1, of which waited for: 1 -> 1; matrix products, arithmetic and copies ran while one was open for 1% -> 1% of each run, Pallas kernels for 0% -> 0%
where the time goes in v1:
time: 125 us
  blocking collectives  81.2 us (65%)
  local copies, waits for them, and re-layouts  15.1 us (12%)
  waiting for transfers between devices  9.73 us (8%)
  other arithmetic  9.57 us (8%)
  starting transfers between devices  5.1 us (4%)
  matrix products  3.47 us (3%)
    all_gather x1, blocking collectives, shards(): gathered = lax.all_gather(hidden, 'tp', axis=0, tiled=True)  33.2 us
    all_gather x1, blocking collectives, shards(): lax.all_gather(jnp.concatenate([down_flat, query_flat, value_flat], axis=...  31.6 us
    all_to_all x1, blocking collectives, shards(): lax.all_to_all(block_terms.reshape(tp_width, tok_rows, block_terms.shape[...  16.3 us
    all_to_all x1, waiting for transfers between devices, shards(): lax.all_to_all(jnp.concatenate([key_send, value_send, latent_send, up_sen...  9.73 us
    select_n x1, other arithmetic, shards(): token_adapter = jnp.take(adapter_choice_list, segment)  5.47 us
    all_to_all x1, starting transfers between devices, shards(): lax.all_to_all(jnp.concatenate([key_send, value_send, latent_send, up_sen...  5.1 us
    unnamed x38, local copies, waits for them, and re-layouts  3.37 us
    all_to_all x2, local copies, waits for them, and re-layouts, shards(): lax.all_to_all(jnp.concatenate([key_send, value_send, latent_send, up_sen...  2.67 us
  transfers between devices with their start and end apart: 1, of which 1 were waited for; matrix products, arithmetic and copies ran while one was open for 1% of the time, Pallas kernels for 0%

profile of v1, /device:TPU:1, one launch (start us, length us, event | category | flops | bytes accessed | tf_op | source)
XLA Modules:
  0.0 124.7 jit_solution(8126652401403183919)
XLA Ops:
  0.1 0.8 copy.133
  0.9 0.8 copy.104
  1.6 0.1 reshape.427
  1.7 0.8 copy.103
  2.6 0.1 reshape.425
  2.7 31.6 %all-gather.1 = bf16[16,1,7680]{2,1,0:T(2,128)(2,1)S(1)} all-gather(bf16[1,1,7680]{2,1,0:T(2,128)(2,1)S(1)} %maximum_bitcast_fusion), channel_id=1, replica_groups=mesh['req'=16,'tp'=32] {'req'}, dimensions={0}, use_global_device_ids=true | all-gather | bytes 261120 | tf_op jit(solution)/shard_map/all_gather | solution.py:94
  34.4 0.7 copy-done.2
  35.1 0.2 reduce-window.4
  35.3 0.7 fusion.53
  36.0 0.1 select_reduce_fusion.1
  36.1 5.5 %and_select_fusion.1 = (s32[64]{0:T(128)S(1)}, f32[64]{0:T(128)}) fusion(s32[64]{0:T(128)S(1)} %get-tuple-element.7, s32[]{:T(128)} %bitcast.18, s32[]{:T(128)} %bitcast.19, s32[]{:T(128)} %bitcast.20, s32[]{:T(128)} %bitcast.21, s32[]{:T(128)} %bitcast.22, s32[]{:T(128)} %bitcast.24, s32[]{:T(128)} %bitcast.23, s32[]{:T(128)} %bitcast.17, ...), kind=kLoop, calls=%fused_computation.95 | loop fusion | flops 1664 | bytes 1056 | tf_op jit(solution)/shard_map/jit(_take)/select_n | solution.py:108
  41.6 0.1 copy.107
  41.7 0.2 copy.108
  41.9 0.7 gather_fusion
  42.6 0.7 copy.109
  43.3 0.2 copy.110
  43.6 0.8 copy.113
  44.4 0.4 reshape.428
  44.8 0.3 copy.105
  45.2 33.2 %all-gather = bf16[32,2,5120]{2,1,0:T(2,128)(2,1)S(1)} all-gather(bf16[1,2,5120]{2,1,0:T(2,128)(2,1)S(1)} %bitcast.145), channel_id=1, replica_groups=mesh['req'=16,'tp'=32] {'tp'}, dimensions={0}, use_global_device_ids=true | all-gather | bytes 675840 | tf_op jit(solution)/shard_map/all_gather | solution.py:111
  78.4 0.2 reshape.528
  78.6 0.2 multiply_reduce_fusion
  78.8 0.5 add_rsqrt_fusion
  79.3 0.9 multiply_convert_fusion
  80.3 0.3 fusion.29
  80.6 0.1 copy.106
  80.7 0.1 reshape.545
  80.8 1.3 %fusion.6 = f32[64,8,4]{0,1,2:T(8,128)S(1)} fusion(bf16[4,8,5120]{2,1,0:T(8,128)(2,1)} %param.19, bf16[64,5120]{1,0:T(8,128)(2,1)S(1)} %multiply_convert_fusion, f32[8,4]{0,1:T(4,128)S(1)} %bitcast.148), kind=kOutput, calls=%fused_computation.19 | convolution fusion | flops 20973568 | bytes 991360 | tf_op jit(solution)/shard_map/tm,ehm->the/dot_general | solution.py:126
  82.1 0.3 convolution_bitcast_fusion.2
  82.4 0.6 gather_fusion.1
  83.0 0.6 gather_fusion.2
  83.6 0.0 copy-done.13
  83.7 0.1 broadcast_select_fusion.1
  83.8 0.1 copy.100
  83.9 0.1 copy.111
  84.0 0.1 copy.102
  84.1 0.1 copy.112
  84.3 1.1 all_to_all.11
  85.4 5.1 %all-to-all-start = ((f32[32,1,3584]{2,1,0:T(1,128)}), f32[32,1,3584]{2,1,0:T(1,128)}, u32[]{:S(2)}, u32[]{:S(2)}) async-start(f32[32,1,3584]{2,1,0:T(1,128)} %all_to_all.11), calls=%async_computation | async-start | bytes 917504 | tf_op jit(solution)/shard_map/all_to_all | solution.py:143
  90.5 0.8 slice.88
  91.4 0.4 convolution_add_fusion.1
  91.8 9.7 %all-to-all-done = f32[32,1,3584]{2,1,0:T(1,128)} async-done(((f32[32,1,3584]{2,1,0:T(1,128)}), f32[32,1,3584]{2,1,0:T(1,128)}, u32[]{:S(2)}, u32[]{:S(2)}) %all-to-all-start) | async-done | bytes 458784 | tf_op jit(solution)/shard_map/all_to_all | solution.py:143
  101.5 1.6 %copy.114 = f32[32,1,3584]{0,2,1:T(8,128)S(1)} copy(f32[32,1,3584]{2,1,0:T(1,128)} %all-to-all-done) | data formatting | bytes 917504 | tf_op jit(solution)/shard_map/all_to_all | solution.py:143
  103.1 0.3 slice_reduce_fusion
  103.4 0.1 bitcast_convert_fusion
  103.6 0.1 convert_element_type.113
  103.7 0.1 fusion.52
  103.8 0.1 copy.123
  103.8 0.1 copy.116
  103.9 0.1 copy.115
  104.0 0.1 copy.119
  104.1 0.1 copy.120
  104.2 0.1 copy.126
  104.3 0.1 copy.125
  104.4 1.0 copy.117
  105.4 0.2 fusion.1
  105.6 0.2 fusion.43
  105.8 0.2 fusion.54
  106.0 0.3 fusion.3
  106.4 0.5 convolution_convert_fusion
  106.9 0.2 reshape.437
  107.2 16.3 %all_to_all.17 = bf16[32,2,5120]{2,1,0:T(2,128)(2,1)S(1)} all-to-all(bf16[32,2,5120]{2,1,0:T(2,128)(2,1)S(1)} %reshape.437), channel_id=1, replica_groups=mesh['req'=16,'tp'=32] {'tp'}, dimensions={0} | all-to-all | bytes 1310720 | tf_op jit(solution)/shard_map/all_to_all | solution.py:212
  123.5 0.5 convert_reduce_fusion
  124.0 0.6 add_convert_fusion
  (55 shorter events, 0.5 us)
Async XLA Ops:
  0.0 106.4 %copy-start = (bf16[128,5120]{1,0:T(8,128)(2,1)S(1)}, bf16[128,5120]{1,0:T(8,128)(2,1)}, u32[]{:S(2)}) copy-start(bf16[128,5120]{1,0:T(8,128)(2,1)} %param.20) | copy-start | bytes 3932164
  0.0 35.1 %copy-start.15 = (s32[1,8]{1,0:T(1,128)S(1)}, s32[1,8]{1,0:T(1,128)}, u32[]{:S(2)}) copy-start(s32[1,8]{1,0:T(1,128)} %param.26) | copy-start | bytes 100
  0.0 35.3 %copy-start.7 = (s32[1,8]{1,0:T(1,128)S(1)}, s32[1,8]{1,0:T(1,128)}, u32[]{:S(2)}) copy-start(s32[1,8]{1,0:T(1,128)} %param.27) | copy-start | bytes 100
  0.0 43.3 %copy-start.12 = (pred[32]{0:T(512)(128)(4,1)}, pred[32]{0:T(512)(128)(4,1)S(1)}, u32[]{:S(2)}) copy-start(pred[32]{0:T(512)(128)(4,1)S(1)} %compare_and_fusion) | copy-start | bytes 100
  34.4 0.7 copy-start.2
  36.1 5.6 %copy-start.10 = (s32[64]{0:T(128)}, s32[64]{0:T(128)S(1)}, u32[]{:S(2)}) copy-start(s32[64]{0:T(128)S(1)} %get-tuple-element.7) | copy-start | bytes 772
  43.5 1.6 %copy-start.5 = (bf16[2,5120]{1,0:T(2,128)(2,1)S(1)}, bf16[2,5120]{1,0:T(2,128)(2,1)}, u32[]{:S(2)}) copy-start(bf16[2,5120]{1,0:T(2,128)(2,1)} %param.15) | copy-start | bytes 61444
  79.3 1.4 %copy-start.8 = (f32[4,8]{1,0:T(4,128)S(1)}, f32[4,8]{1,0:T(4,128)}, u32[]{:S(2)}) copy-start(f32[4,8]{1,0:T(4,128)} %param.22) | copy-start | bytes 388
  80.3 1.8 %copy-start.4 = (bf16[4,8,5120]{2,1,0:T(8,128)(2,1)S(1)}, bf16[4,8,5120]{2,1,0:T(8,128)(2,1)}, u32[]{:S(2)}) copy-start(bf16[4,8,5120]{2,1,0:T(8,128)(2,1)} %param.18) | copy-start | bytes 983044
  83.0 0.7 copy-start.13
  83.0 1.2 copy-start.3
  84.2 7.2 %copy-start.1 = (bf16[5120,128]{1,0:T(8,128)(2,1)S(1)}, bf16[5120,128]{1,0:T(8,128)(2,1)}, u32[]{:S(2)}) copy-start(bf16[5120,128]{1,0:T(8,128)(2,1)} %param.17) | copy-start | bytes 3932164
  84.2 7.2 %copy-start.14 = (f32[128]{0:T(128)S(1)}, f32[128]{0:T(128)}, u32[]{:S(2)}) copy-start(f32[128]{0:T(128)} %param.21) | copy-start | bytes 1540
  85.4 16.1 %all-to-all-start = ((f32[32,1,3584]{2,1,0:T(1,128)}), f32[32,1,3584]{2,1,0:T(1,128)}, u32[]{:S(2)}, u32[]{:S(2)}) async-start(f32[32,1,3584]{2,1,0:T(1,128)} %all_to_all.11), calls=%async_computation | async-start | bytes 917504 | tf_op jit(solution)/shard_map/all_to_all | solution.py:143
  103.5 2.0 %copy-start.9 = (f32[64]{0:T(128)S(1)}, f32[64]{0:T(128)}, u32[]{:S(2)}) copy-start(f32[64]{0:T(128)} %get-tuple-element.33) | copy-start | bytes 772
  103.6 2.2 %copy-start.11 = (s32[64]{0:T(128)S(1)}, s32[64]{0:T(128)}, u32[]{:S(2)}) copy-start(s32[64]{0:T(128)} %copy-done.10) | copy-start | bytes 772
  107.2 16.9 %copy-start.6 = (bf16[2,5120]{1,0:T(2,128)(2,1)S(1)}, bf16[2,5120]{1,0:T(2,128)(2,1)}, u32[]{:S(2)}) copy-start(bf16[2,5120]{1,0:T(2,128)(2,1)} %param.15) | copy-start | bytes 61444

commit v2 on v1

--- a/solution.py
+++ b/solution.py
@@ -47,6 +47,28 @@
         [lower_half * cosine - upper_half * sines, upper_half * cosine + lower_half * sines],
         axis=-1,
     )
+
+
+def ring_gather(x, axis, n):
+    parts = [x] + [lax.ppermute(x, axis, [(i, (i - k) % n) for i in range(n)]) for k in range(1, n)]
+    rel = jnp.stack(parts)
+    me = lax.axis_index(axis)
+    return lax.dynamic_slice_in_dim(jnp.concatenate([rel, rel]), n - me, n, 0)
+
+
+def ring_deliver(send, axis, n):
+    me = lax.axis_index(axis)
+    rot = lax.dynamic_slice_in_dim(jnp.concatenate([send, send]), me, n, 0)
+    parts = [rot[0]] + [
+        lax.ppermute(rot[k], axis, [(i, (i + k) % n) for i in range(n)]) for k in range(1, n)
+    ]
+    return jnp.stack(parts)
+
+
+def source_order(rel, axis, n):
+    me = lax.axis_index(axis)
+    both = jnp.concatenate([rel, rel])
+    return jnp.flip(lax.dynamic_slice_in_dim(both, me + 1, n, 0), axis=0)
 
 
 def attend(query_rot, key_rot, value_head, segment):
@@ -91,8 +113,9 @@
     down_flat = adapter_down_maps.reshape(1, -1)
     query_flat = adapter_query_up.reshape(1, -1)
     value_flat = adapter_value_up.reshape(1, -1)
-    bank = lax.all_gather(
-        jnp.concatenate([down_flat, query_flat, value_flat], axis=1), "req", axis=0, tiled=True
+    req_width = lax.axis_size("req")
+    bank = ring_gather(
+        jnp.concatenate([down_flat, query_flat, value_flat], axis=1)[0], "req", req_width
     )
     adapter_total = bank.shape[0]
     n_down, n_query = down_flat.shape[1], query_flat.shape[1]
@@ -108,7 +131,7 @@
     token_adapter = jnp.take(adapter_choice_list, segment)
     adapter_pick = token_adapter[:, None] == jnp.arange(adapter_total, dtype=jnp.int32)[None, :]
 
-    gathered = lax.all_gather(hidden, "tp", axis=0, tiled=True)
+    gathered = ring_gather(hidden, "tp", tp_width).reshape(group_tokens, hidden.shape[1])
     normalized_input = rms_rows(gathered, input_norm_gain)
 
     own_features = lax.dynamic_slice_in_dim(
@@ -140,12 +163,12 @@
         .reshape(tp_width, -1)
     )
     n_key, n_value, n_latent = key_send.shape[1], value_send.shape[1], latent_send.shape[1]
-    received = lax.all_to_all(
-        jnp.concatenate([key_send, value_send, latent_send, up_send], axis=1),
+    received = source_order(
+        ring_deliver(
+            jnp.concatenate([key_send, value_send, latent_send, up_send], axis=1), "tp", tp_width
+        ),
         "tp",
-        0,
-        0,
-        tiled=True,
+        tp_width,
     )
     key_head = (
         received[:, :n_key]
@@ -209,8 +232,8 @@
     block_terms = jnp.dot(mixed_heads, output_weight, preferred_element_type=jnp.float32).astype(
         jnp.bfloat16
     )
-    owner_terms = lax.all_to_all(
-        block_terms.reshape(tp_width, tok_rows, block_terms.shape[-1]), "tp", 0, 0, tiled=True
+    owner_terms = ring_deliver(
+        block_terms.reshape(tp_width, tok_rows, block_terms.shape[-1]), "tp", tp_width
     )
     projected = jnp.sum(owner_terms.astype(jnp.float32), axis=0)
     return (hidden.astype(jnp.float32) + projected).astype(jnp.bfloat16)

time: 125 us -> 837 us (6.70)
  starting transfers between devices: 5.1 us -> 607 us
  waiting for transfers between devices: 9.73 us -> 157 us
  blocking collectives: 81.2 us -> 0 us
  local copies, waits for them, and re-layouts: 15.1 us -> 43.1 us
    ppermute x0 -> x108, starting transfers between devices: none -> 607 us  [the longest x46 375 us: ring_gather(): lax.ppermute(x, axis, [(i, (i - k) % n) for i in range(n)])]
    ppermute x0 -> x108, waiting for transfers between devices: none -> 157 us  [the longest x62 98.5 us: ring_deliver(): lax.ppermute(rot[k], axis, [(i, (i + k) % n) for i in range(n)])]
    all_gather x2 -> x0, blocking collectives: 64.9 us -> none  [the longest x1 33.2 us: shards(): gathered = lax.all_gather(hidden, 'tp', axis=0, tiled=True)]
    all_to_all x1 -> x0, blocking collectives: 16.3 us -> none  [shards(): lax.all_to_all(block_terms.reshape(tp_width, tok_rows, block_terms.shape[...]
    unnamed x38 -> x215, local copies, waits for them, and re-layouts: 3.37 us -> 14.5 us
    all_to_all x1 -> x0, waiting for transfers between devices: 9.73 us -> none  [shards(): lax.all_to_all(jnp.concatenate([key_send, value_send, latent_send, up_sen...]
  transfers between devices with their start and end apart: 1 -> 108, of which waited for: 1 -> 51; matrix products, arithmetic and copies ran while one was open for 1% -> 4% of each run, Pallas kernels for 0% -> 0%
where the time goes in v2:
time: 837 us; the launch traced here: 830 us
  starting transfers between devices  607 us (73%)
  waiting for transfers between devices  157 us (19%)
  local copies, waits for them, and re-layouts  43.1 us (5%)
  other arithmetic  16.7 us (2%)
    ppermute x46, starting transfers between devices, ring_gather(): lax.ppermute(x, axis, [(i, (i - k) % n) for i in range(n)])  375 us
    ppermute x62, starting transfers between devices, ring_deliver(): lax.ppermute(rot[k], axis, [(i, (i + k) % n) for i in range(n)])  231 us
    ppermute x62, waiting for transfers between devices, ring_deliver(): lax.ppermute(rot[k], axis, [(i, (i + k) % n) for i in range(n)])  98.5 us
    ppermute x46, waiting for transfers between devices, ring_gather(): lax.ppermute(x, axis, [(i, (i - k) % n) for i in range(n)])  58.2 us
  transfers between devices with their start and end apart: 108, of which 51 were waited for; matrix products, arithmetic and copies ran while one was open for 4% of the time, Pallas kernels for 0%

profile of v2, /device:TPU:1, one launch (start us, length us, event | category | flops | bytes accessed | tf_op | source)
XLA Modules:
  0.0 830.3 jit_solution(11038237729714291018)
XLA Ops:
  2.8 4.4 collective-permute-start.45
  7.2 4.9 collective-permute-start.44
  12.1 7.5 collective-permute-start.43
  19.5 7.0 collective-permute-start.42
  26.6 4.5 collective-permute-start.41
  34.3 5.6 and_select_fusion.1
  41.2 14.5 %collective-permute-start.40 = (bf16[7680]{0:T(1024)(128)(2,1)S(1)}, bf16[7680]{0:T(1024)(128)(2,1)S(1)}, u32[]{:S(2)}, u32[]{:S(2)}) collective-permute-start(bf16[7680]{0:T(1024)(128)(2,1)S(1)} %reduce.4), channel_id=1, source_target_pairs={{0,192},{32,224},{64,256},{96,288},{128,320},{160,352},{192,384},{... | collective-permute-start | bytes 46088 | tf_op jit(solution)/shard_map/ppermute | solution.py:53
  55.8 19.0 %collective-permute-start.39 = (bf16[7680]{0:T(1024)(128)(2,1)S(1)}, bf16[7680]{0:T(1024)(128)(2,1)S(1)}, u32[]{:S(2)}, u32[]{:S(2)}) collective-permute-start(bf16[7680]{0:T(1024)(128)(2,1)S(1)} %reduce.4), channel_id=1, source_target_pairs={{0,224},{32,256},{64,288},{96,320},{128,352},{160,384},{192,416},{... | collective-permute-start | bytes 46088 | tf_op jit(solution)/shard_map/ppermute | solution.py:53
  74.8 19.0 %collective-permute-start.38 = (bf16[7680]{0:T(1024)(128)(2,1)S(1)}, bf16[7680]{0:T(1024)(128)(2,1)S(1)}, u32[]{:S(2)}, u32[]{:S(2)}) collective-permute-start(bf16[7680]{0:T(1024)(128)(2,1)S(1)} %reduce.4), channel_id=1, source_target_pairs={{0,256},{32,288},{64,320},{96,352},{128,384},{160,416},{192,448},{... | collective-permute-start | bytes 46088 | tf_op jit(solution)/shard_map/ppermute | solution.py:53
  93.8 19.0 %collective-permute-start.37 = (bf16[7680]{0:T(1024)(128)(2,1)S(1)}, bf16[7680]{0:T(1024)(128)(2,1)S(1)}, u32[]{:S(2)}, u32[]{:S(2)}) collective-permute-start(bf16[7680]{0:T(1024)(128)(2,1)S(1)} %reduce.4), channel_id=1, source_target_pairs={{0,288},{32,320},{64,352},{96,384},{128,416},{160,448},{192,480},{... | collective-permute-start | bytes 46088 | tf_op jit(solution)/shard_map/ppermute | solution.py:53
  112.9 19.0 %collective-permute-start.36 = (bf16[7680]{0:T(1024)(128)(2,1)S(1)}, bf16[7680]{0:T(1024)(128)(2,1)S(1)}, u32[]{:S(2)}, u32[]{:S(2)}) collective-permute-start(bf16[7680]{0:T(1024)(128)(2,1)S(1)} %reduce.4), channel_id=1, source_target_pairs={{0,320},{32,352},{64,384},{96,416},{128,448},{160,480},{192,0},{22... | collective-permute-start | bytes 46088 | tf_op jit(solution)/shard_map/ppermute | solution.py:53
  132.5 19.0 %collective-permute-start.35 = (bf16[7680]{0:T(1024)(128)(2,1)S(1)}, bf16[7680]{0:T(1024)(128)(2,1)S(1)}, u32[]{:S(2)}, u32[]{:S(2)}) collective-permute-start(bf16[7680]{0:T(1024)(128)(2,1)S(1)} %reduce.4), channel_id=1, source_target_pairs={{0,352},{32,384},{64,416},{96,448},{128,480},{160,0},{192,32},{224... | collective-permute-start | bytes 46088 | tf_op jit(solution)/shard_map/ppermute | solution.py:53
  151.5 19.0 %collective-permute-start.34 = (bf16[7680]{0:T(1024)(128)(2,1)S(1)}, bf16[7680]{0:T(1024)(128)(2,1)S(1)}, u32[]{:S(2)}, u32[]{:S(2)}) collective-permute-start(bf16[7680]{0:T(1024)(128)(2,1)S(1)} %reduce.4), channel_id=1, source_target_pairs={{0,384},{32,416},{64,448},{96,480},{128,0},{160,32},{192,64},{224,... | collective-permute-start | bytes 46088 | tf_op jit(solution)/shard_map/ppermute | solution.py:53
  170.5 19.0 %collective-permute-start.33 = (bf16[7680]{0:T(1024)(128)(2,1)S(1)}, bf16[7680]{0:T(1024)(128)(2,1)S(1)}, u32[]{:S(2)}, u32[]{:S(2)}) collective-permute-start(bf16[7680]{0:T(1024)(128)(2,1)S(1)} %reduce.4), channel_id=1, source_target_pairs={{0,416},{32,448},{64,480},{96,0},{128,32},{160,64},{192,96},{224,1... | collective-permute-start | bytes 46088 | tf_op jit(solution)/shard_map/ppermute | solution.py:53
  189.5 19.0 %collective-permute-start.32 = (bf16[7680]{0:T(1024)(128)(2,1)S(1)}, bf16[7680]{0:T(1024)(128)(2,1)S(1)}, u32[]{:S(2)}, u32[]{:S(2)}) collective-permute-start(bf16[7680]{0:T(1024)(128)(2,1)S(1)} %reduce.4), channel_id=1, source_target_pairs={{0,448},{32,480},{64,0},{96,32},{128,64},{160,96},{192,128},{224,1... | collective-permute-start | bytes 46088 | tf_op jit(solution)/shard_map/ppermute | solution.py:53
  208.6 19.0 %collective-permute-start.31 = (bf16[7680]{0:T(1024)(128)(2,1)S(1)}, bf16[7680]{0:T(1024)(128)(2,1)S(1)}, u32[]{:S(2)}, u32[]{:S(2)}) collective-permute-start(bf16[7680]{0:T(1024)(128)(2,1)S(1)} %reduce.4), channel_id=1, source_target_pairs={{0,480},{32,0},{64,32},{96,64},{128,96},{160,128},{192,160},{224,1... | collective-permute-start | bytes 46088 | tf_op jit(solution)/shard_map/ppermute | solution.py:53
  227.9 5.1 collective-permute-start.28
  261.2 8.1 collective-permute-start.2
  276.6 6.1 collective-permute-start.4
  290.2 7.7 collective-permute-start.6
  304.9 9.4 %collective-permute-start.8 = (bf16[2,5120]{1,0:T(2,128)(2,1)}, bf16[2,5120]{1,0:T(2,128)(2,1)S(1)}, u32[]{:S(2)}, u32[]{:S(2)}) collective-permute-start(bf16[2,5120]{1,0:T(2,128)(2,1)} %param.15), channel_id=1, source_target_pairs={{0,23},{1,24},{2,25},{3,26},{4,27},{5,28},{6,29},{7,30},{8,31},{9,... | collective-permute-start | bytes 61448 | tf_op jit(solution)/shard_map/ppermute | solution.py:53
  315.4 7.2 collective-permute-start.9
  323.8 8.0 collective-permute-start.10
  332.9 6.4 collective-permute-start.11
  340.4 7.1 collective-permute-start.12
  348.6 6.7 collective-permute-start.13
  356.6 8.7 %collective-permute-start.14 = (bf16[2,5120]{1,0:T(2,128)(2,1)}, bf16[2,5120]{1,0:T(2,128)(2,1)S(1)}, u32[]{:S(2)}, u32[]{:S(2)}) collective-permute-start(bf16[2,5120]{1,0:T(2,128)(2,1)} %param.15), channel_id=1, source_target_pairs={{0,17},{1,18},{2,19},{3,20},{4,21},{5,22},{6,23},{7,24},{8,25},{9,... | collective-permute-start | bytes 61448 | tf_op jit(solution)/shard_map/ppermute | solution.py:53
  375.9 6.9 collective-permute-start.16
  383.9 5.7 collective-permute-start.17
  391.0 7.1 collective-permute-start.18
  400.4 5.5 collective-permute-start.19
  409.1 5.4 collective-permute-start.20
  420.4 6.0 collective-permute-done.21
  429.3 5.1 collective-permute-done.22
  440.4 6.2 collective-permute-start.24
  455.9 5.8 collective-permute-done.29
  488.3 5.3 collective-permute-start.54
  498.7 7.2 collective-permute-start.51
  524.1 5.7 collective-permute-start.75
  529.8 4.9 collective-permute-start.74
  557.7 4.7 collective-permute-start.66
  562.4 4.8 collective-permute-start.65
  576.0 4.5 collective-permute-start.62
  586.7 4.6 collective-permute-start.59
  614.3 5.4 collective-permute-start.106
  623.3 5.6 collective-permute-start.104
  630.8 5.9 collective-permute-done.78
  638.7 6.5 collective-permute-done.79
  647.1 6.2 collective-permute-done.80
  655.2 6.8 collective-permute-done.81
  663.9 4.7 collective-permute-done.82
  670.5 5.3 collective-permute-done.83
  689.8 6.2 collective-permute-done.86
  697.9 6.8 collective-permute-done.87
  715.7 7.4 collective-permute-done.89
  725.0 5.0 collective-permute-done.90
  734.0 4.7 collective-permute-done.91
  738.7 4.9 collective-permute-start.92
  744.7 6.3 collective-permute-start.93
  759.3 7.2 collective-permute-start.95
  774.9 9.0 %collective-permute-start.97 = (bf16[2,5120]{1,0:T(2,128)(2,1)S(1)}, bf16[2,5120]{1,0:T(2,128)(2,1)S(1)}, u32[]{:S(2)}, u32[]{:S(2)}) collective-permute-start(bf16[2,5120]{1,0:T(2,128)(2,1)S(1)} %get-tuple-element.49), channel_id=1, source_target_pairs={{0,21},{1,22},{2,23},{3,24},{4,25},{5,26},{6,27},{7,28},{8,29},{9,... | collective-permute-start | bytes 61448 | tf_op jit(solution)/shard_map/ppermute | solution.py:63
  790.9 10.4 %collective-permute-start.99 = (bf16[2,5120]{1,0:T(2,128)(2,1)S(1)}, bf16[2,5120]{1,0:T(2,128)(2,1)S(1)}, u32[]{:S(2)}, u32[]{:S(2)}) collective-permute-start(bf16[2,5120]{1,0:T(2,128)(2,1)S(1)} %get-tuple-element.47), channel_id=1, source_target_pairs={{0,23},{1,24},{2,25},{3,26},{4,27},{5,28},{6,29},{7,30},{8,31},{9,... | collective-permute-start | bytes 61448 | tf_op jit(solution)/shard_map/ppermute | solution.py:63
  811.9 5.1 collective-permute-start.102
  818.6 9.4 %collective-permute-start.103 = (bf16[2,5120]{1,0:T(2,128)(2,1)S(1)}, bf16[2,5120]{1,0:T(2,128)(2,1)S(1)}, u32[]{:S(2)}, u32[]{:S(2)}) collective-permute-start(bf16[2,5120]{1,0:T(2,128)(2,1)S(1)} %get-tuple-element.43), channel_id=1, source_target_pairs={{0,27},{1,28},{2,29},{3,30},{4,31},{5,0},{6,1},{7,2},{8,3},{9,4},{... | collective-permute-start | bytes 61448 | tf_op jit(solution)/shard_map/ppermute | solution.py:63
  (505 shorter events, 303.6 us)
Async XLA Ops:
  2.8 38.5 %collective-permute-start.45 = (bf16[7680]{0:T(1024)(128)(2,1)S(1)}, bf16[7680]{0:T(1024)(128)(2,1)S(1)}, u32[]{:S(2)}, u32[]{:S(2)}) collective-permute-start(bf16[7680]{0:T(1024)(128)(2,1)S(1)} %reduce.4), channel_id=1, source_target_pairs={{0,32},{32,64},{64,96},{96,128},{128,160},{160,192},{192,224},{224... | collective-permute-start | bytes 46088 | tf_op jit(solution)/shard_map/ppermute | solution.py:53
  7.2 48.6 %collective-permute-start.44 = (bf16[7680]{0:T(1024)(128)(2,1)S(1)}, bf16[7680]{0:T(1024)(128)(2,1)S(1)}, u32[]{:S(2)}, u32[]{:S(2)}) collective-permute-start(bf16[7680]{0:T(1024)(128)(2,1)S(1)} %reduce.4), channel_id=1, source_target_pairs={{0,64},{32,96},{64,128},{96,160},{128,192},{160,224},{192,256},{22... | collective-permute-start | bytes 46088 | tf_op jit(solution)/shard_map/ppermute | solution.py:53
  12.1 62.8 %collective-permute-start.43 = (bf16[7680]{0:T(1024)(128)(2,1)S(1)}, bf16[7680]{0:T(1024)(128)(2,1)S(1)}, u32[]{:S(2)}, u32[]{:S(2)}) collective-permute-start(bf16[7680]{0:T(1024)(128)(2,1)S(1)} %reduce.4), channel_id=1, source_target_pairs={{0,96},{32,128},{64,160},{96,192},{128,224},{160,256},{192,288},{2... | collective-permute-start | bytes 46088 | tf_op jit(solution)/shard_map/ppermute | solution.py:53
  19.5 74.3 %collective-permute-start.42 = (bf16[7680]{0:T(1024)(128)(2,1)S(1)}, bf16[7680]{0:T(1024)(128)(2,1)S(1)}, u32[]{:S(2)}, u32[]{:S(2)}) collective-permute-start(bf16[7680]{0:T(1024)(128)(2,1)S(1)} %reduce.4), channel_id=1, source_target_pairs={{0,128},{32,160},{64,192},{96,224},{128,256},{160,288},{192,320},{... | collective-permute-start | bytes 46088 | tf_op jit(solution)/shard_map/ppermute | solution.py:53
  26.6 86.3 %collective-permute-start.41 = (bf16[7680]{0:T(1024)(128)(2,1)S(1)}, bf16[7680]{0:T(1024)(128)(2,1)S(1)}, u32[]{:S(2)}, u32[]{:S(2)}) collective-permute-start(bf16[7680]{0:T(1024)(128)(2,1)S(1)} %reduce.4), channel_id=1, source_target_pairs={{0,160},{32,192},{64,224},{96,256},{128,288},{160,320},{192,352},{... | collective-permute-start | bytes 46088 | tf_op jit(solution)/shard_map/ppermute | solution.py:53
  41.2 91.2 %collective-permute-start.40 = (bf16[7680]{0:T(1024)(128)(2,1)S(1)}, bf16[7680]{0:T(1024)(128)(2,1)S(1)}, u32[]{:S(2)}, u32[]{:S(2)}) collective-permute-start(bf16[7680]{0:T(1024)(128)(2,1)S(1)} %reduce.4), channel_id=1, source_target_pairs={{0,192},{32,224},{64,256},{96,288},{128,320},{160,352},{192,384},{... | collective-permute-start | bytes 46088 | tf_op jit(solution)/shard_map/ppermute | solution.py:53
  55.8 95.7 %collective-permute-start.39 = (bf16[7680]{0:T(1024)(128)(2,1)S(1)}, bf16[7680]{0:T(1024)(128)(2,1)S(1)}, u32[]{:S(2)}, u32[]{:S(2)}) collective-permute-start(bf16[7680]{0:T(1024)(128)(2,1)S(1)} %reduce.4), channel_id=1, source_target_pairs={{0,224},{32,256},{64,288},{96,320},{128,352},{160,384},{192,416},{... | collective-permute-start | bytes 46088 | tf_op jit(solution)/shard_map/ppermute | solution.py:53
  74.8 95.7 %collective-permute-start.38 = (bf16[7680]{0:T(1024)(128)(2,1)S(1)}, bf16[7680]{0:T(1024)(128)(2,1)S(1)}, u32[]{:S(2)}, u32[]{:S(2)}) collective-permute-start(bf16[7680]{0:T(1024)(128)(2,1)S(1)} %reduce.4), channel_id=1, source_target_pairs={{0,256},{32,288},{64,320},{96,352},{128,384},{160,416},{192,448},{... | collective-permute-start | bytes 46088 | tf_op jit(solution)/shard_map/ppermute | solution.py:53
  93.8 95.7 %collective-permute-start.37 = (bf16[7680]{0:T(1024)(128)(2,1)S(1)}, bf16[7680]{0:T(1024)(128)(2,1)S(1)}, u32[]{:S(2)}, u32[]{:S(2)}) collective-permute-start(bf16[7680]{0:T(1024)(128)(2,1)S(1)} %reduce.4), channel_id=1, source_target_pairs={{0,288},{32,320},{64,352},{96,384},{128,416},{160,448},{192,480},{... | collective-permute-start | bytes 46088 | tf_op jit(solution)/shard_map/ppermute | solution.py:53
  112.9 95.7 %collective-permute-start.36 = (bf16[7680]{0:T(1024)(128)(2,1)S(1)}, bf16[7680]{0:T(1024)(128)(2,1)S(1)}, u32[]{:S(2)}, u32[]{:S(2)}) collective-permute-start(bf16[7680]{0:T(1024)(128)(2,1)S(1)} %reduce.4), channel_id=1, source_target_pairs={{0,320},{32,352},{64,384},{96,416},{128,448},{160,480},{192,0},{22... | collective-permute-start | bytes 46088 | tf_op jit(solution)/shard_map/ppermute | solution.py:53
  132.5 95.4 %collective-permute-start.35 = (bf16[7680]{0:T(1024)(128)(2,1)S(1)}, bf16[7680]{0:T(1024)(128)(2,1)S(1)}, u32[]{:S(2)}, u32[]{:S(2)}) collective-permute-start(bf16[7680]{0:T(1024)(128)(2,1)S(1)} %reduce.4), channel_id=1, source_target_pairs={{0,352},{32,384},{64,416},{96,448},{128,480},{160,0},{192,32},{224... | collective-permute-start | bytes 46088 | tf_op jit(solution)/shard_map/ppermute | solution.py:53
  151.5 81.5 %collective-permute-start.34 = (bf16[7680]{0:T(1024)(128)(2,1)S(1)}, bf16[7680]{0:T(1024)(128)(2,1)S(1)}, u32[]{:S(2)}, u32[]{:S(2)}) collective-permute-start(bf16[7680]{0:T(1024)(128)(2,1)S(1)} %reduce.4), channel_id=1, source_target_pairs={{0,384},{32,416},{64,448},{96,480},{128,0},{160,32},{192,64},{224,... | collective-permute-start | bytes 46088 | tf_op jit(solution)/shard_map/ppermute | solution.py:53
  170.5 65.6 %collective-permute-start.33 = (bf16[7680]{0:T(1024)(128)(2,1)S(1)}, bf16[7680]{0:T(1024)(128)(2,1)S(1)}, u32[]{:S(2)}, u32[]{:S(2)}) collective-permute-start(bf16[7680]{0:T(1024)(128)(2,1)S(1)} %reduce.4), channel_id=1, source_target_pairs={{0,416},{32,448},{64,480},{96,0},{128,32},{160,64},{192,96},{224,1... | collective-permute-start | bytes 46088 | tf_op jit(solution)/shard_map/ppermute | solution.py:53
  189.5 51.2 %collective-permute-start.32 = (bf16[7680]{0:T(1024)(128)(2,1)S(1)}, bf16[7680]{0:T(1024)(128)(2,1)S(1)}, u32[]{:S(2)}, u32[]{:S(2)}) collective-permute-start(bf16[7680]{0:T(1024)(128)(2,1)S(1)} %reduce.4), channel_id=1, source_target_pairs={{0,448},{32,480},{64,0},{96,32},{128,64},{160,96},{192,128},{224,1... | collective-permute-start | bytes 46088 | tf_op jit(solution)/shard_map/ppermute | solution.py:53
  208.6 35.3 %collective-permute-start.31 = (bf16[7680]{0:T(1024)(128)(2,1)S(1)}, bf16[7680]{0:T(1024)(128)(2,1)S(1)}, u32[]{:S(2)}, u32[]{:S(2)}) collective-permute-start(bf16[7680]{0:T(1024)(128)(2,1)S(1)} %reduce.4), channel_id=1, source_target_pairs={{0,480},{32,0},{64,32},{96,64},{128,96},{160,128},{192,160},{224,1... | collective-permute-start | bytes 46088 | tf_op jit(solution)/shard_map/ppermute | solution.py:53
  227.9 227.3 %collective-permute-start.28 = (bf16[2,5120]{1,0:T(2,128)(2,1)}, bf16[2,5120]{1,0:T(2,128)(2,1)}, u32[]{:S(2)}, u32[]{:S(2)}) collective-permute-start(bf16[2,5120]{1,0:T(2,128)(2,1)} %param.15), channel_id=1, source_target_pairs={{0,3},{1,4},{2,5},{3,6},{4,7},{5,8},{6,9},{7,10},{8,11},{9,12},{10... | collective-permute-start | bytes 61448 | tf_op jit(solution)/shard_map/ppermute | solution.py:53
  233.0 221.4 %collective-permute-start.27 = (bf16[2,5120]{1,0:T(2,128)(2,1)}, bf16[2,5120]{1,0:T(2,128)(2,1)}, u32[]{:S(2)}, u32[]{:S(2)}) collective-permute-start(bf16[2,5120]{1,0:T(2,128)(2,1)} %param.15), channel_id=1, source_target_pairs={{0,4},{1,5},{2,6},{3,7},{4,8},{5,9},{6,10},{7,11},{8,12},{9,13},{1... | collective-permute-start | bytes 61448 | tf_op jit(solution)/shard_map/ppermute | solution.py:53
  236.1 217.5 %collective-permute-start.26 = (bf16[2,5120]{1,0:T(2,128)(2,1)}, bf16[2,5120]{1,0:T(2,128)(2,1)}, u32[]{:S(2)}, u32[]{:S(2)}) collective-permute-start(bf16[2,5120]{1,0:T(2,128)(2,1)} %param.15), channel_id=1, source_target_pairs={{0,5},{1,6},{2,7},{3,8},{4,9},{5,10},{6,11},{7,12},{8,13},{9,14},{... | collective-permute-start | bytes 61448 | tf_op jit(solution)/shard_map/ppermute | solution.py:53
  240.8 210.0 %collective-permute-start.25 = (bf16[2,5120]{1,0:T(2,128)(2,1)}, bf16[2,5120]{1,0:T(2,128)(2,1)}, u32[]{:S(2)}, u32[]{:S(2)}) collective-permute-start(bf16[2,5120]{1,0:T(2,128)(2,1)} %param.15), channel_id=1, source_target_pairs={{0,6},{1,7},{2,8},{3,9},{4,10},{5,11},{6,12},{7,13},{8,14},{9,15},... | collective-permute-start | bytes 61448 | tf_op jit(solution)/shard_map/ppermute | solution.py:53
  243.9 12.5 %collective-permute-start = (bf16[2,5120]{1,0:T(2,128)(2,1)}, bf16[2,5120]{1,0:T(2,128)(2,1)}, u32[]{:S(2)}, u32[]{:S(2)}) collective-permute-start(bf16[2,5120]{1,0:T(2,128)(2,1)} %param.15), channel_id=1, source_target_pairs={{0,31},{1,0},{2,1},{3,2},{4,3},{5,4},{6,5},{7,6},{8,7},{9,8},{10,9... | collective-permute-start | bytes 61448 | tf_op jit(solution)/shard_map/ppermute | solution.py:53
  304.9 10.5 %collective-permute-start.8 = (bf16[2,5120]{1,0:T(2,128)(2,1)}, bf16[2,5120]{1,0:T(2,128)(2,1)S(1)}, u32[]{:S(2)}, u32[]{:S(2)}) collective-permute-start(bf16[2,5120]{1,0:T(2,128)(2,1)} %param.15), channel_id=1, source_target_pairs={{0,23},{1,24},{2,25},{3,26},{4,27},{5,28},{6,29},{7,30},{8,31},{9,... | collective-permute-start | bytes 61448 | tf_op jit(solution)/shard_map/ppermute | solution.py:53
  356.6 13.1 %collective-permute-start.14 = (bf16[2,5120]{1,0:T(2,128)(2,1)}, bf16[2,5120]{1,0:T(2,128)(2,1)S(1)}, u32[]{:S(2)}, u32[]{:S(2)}) collective-permute-start(bf16[2,5120]{1,0:T(2,128)(2,1)} %param.15), channel_id=1, source_target_pairs={{0,17},{1,18},{2,19},{3,20},{4,21},{5,22},{6,23},{7,24},{8,25},{9,... | collective-permute-start | bytes 61448 | tf_op jit(solution)/shard_map/ppermute | solution.py:53
  448.0 13.7 %collective-permute-start.30 = (bf16[2,5120]{1,0:T(2,128)(2,1)}, bf16[2,5120]{1,0:T(2,128)(2,1)S(1)}, u32[]{:S(2)}, u32[]{:S(2)}) collective-permute-start(bf16[2,5120]{1,0:T(2,128)(2,1)} %param.15), channel_id=1, source_target_pairs={{0,1},{1,2},{2,3},{3,4},{4,5},{5,6},{6,7},{7,8},{8,9},{9,10},{10,1... | collective-permute-start | bytes 61448 | tf_op jit(solution)/shard_map/ppermute | solution.py:53
  450.8 10.9 %collective-permute-start.29 = (bf16[2,5120]{1,0:T(2,128)(2,1)}, bf16[2,5120]{1,0:T(2,128)(2,1)S(1)}, u32[]{:S(2)}, u32[]{:S(2)}) collective-permute-start(bf16[2,5120]{1,0:T(2,128)(2,1)} %param.15), channel_id=1, source_target_pairs={{0,2},{1,3},{2,4},{3,5},{4,6},{5,7},{6,8},{7,9},{8,10},{9,11},{10,... | collective-permute-start | bytes 61448 | tf_op jit(solution)/shard_map/ppermute | solution.py:53
  479.8 16.1 %collective-permute-start.57 = (f32[3584]{0:T(1024)S(1)}, f32[3584]{0:T(1024)S(1)}, u32[]{:S(2)}, u32[]{:S(2)}) collective-permute-start(f32[3584]{0:T(1024)S(1)} %get-tuple-element.25), channel_id=1, source_target_pairs={{0,12},{1,13},{2,14},{3,15},{4,16},{5,17},{6,18},{7,19},{8,20},{9,... | collective-permute-start | bytes 43016 | tf_op jit(solution)/shard_map/ppermute | solution.py:63
  482.4 16.3 %collective-permute-start.56 = (f32[3584]{0:T(1024)S(1)}, f32[3584]{0:T(1024)S(1)}, u32[]{:S(2)}, u32[]{:S(2)}) collective-permute-start(f32[3584]{0:T(1024)S(1)} %get-tuple-element.26), channel_id=1, source_target_pairs={{0,11},{1,12},{2,13},{3,14},{4,15},{5,16},{6,17},{7,18},{8,19},{9,... | collective-permute-start | bytes 43016 | tf_op jit(solution)/shard_map/ppermute | solution.py:63
  486.4 19.5 %collective-permute-start.55 = (f32[3584]{0:T(1024)S(1)}, f32[3584]{0:T(1024)S(1)}, u32[]{:S(2)}, u32[]{:S(2)}) collective-permute-start(f32[3584]{0:T(1024)S(1)} %get-tuple-element.27), channel_id=1, source_target_pairs={{0,10},{1,11},{2,12},{3,13},{4,14},{5,15},{6,16},{7,17},{8,18},{9,... | collective-permute-start | bytes 43016 | tf_op jit(solution)/shard_map/ppermute | solution.py:63
  488.3 20.0 %collective-permute-start.54 = (f32[3584]{0:T(1024)S(1)}, f32[3584]{0:T(1024)S(1)}, u32[]{:S(2)}, u32[]{:S(2)}) collective-permute-start(f32[3584]{0:T(1024)S(1)} %get-tuple-element.28), channel_id=1, source_target_pairs={{0,9},{1,10},{2,11},{3,12},{4,13},{5,14},{6,15},{7,16},{8,17},{9,1... | collective-permute-start | bytes 43016 | tf_op jit(solution)/shard_map/ppermute | solution.py:63
  493.6 18.9 %collective-permute-start.53 = (f32[3584]{0:T(1024)S(1)}, f32[3584]{0:T(1024)S(1)}, u32[]{:S(2)}, u32[]{:S(2)}) collective-permute-start(f32[3584]{0:T(1024)S(1)} %get-tuple-element.29), channel_id=1, source_target_pairs={{0,8},{1,9},{2,10},{3,11},{4,12},{5,13},{6,14},{7,15},{8,16},{9,17... | collective-permute-start | bytes 43016 | tf_op jit(solution)/shard_map/ppermute | solution.py:63
  495.9 19.1 %collective-permute-start.52 = (f32[3584]{0:T(1024)S(1)}, f32[3584]{0:T(1024)S(1)}, u32[]{:S(2)}, u32[]{:S(2)}) collective-permute-start(f32[3584]{0:T(1024)S(1)} %get-tuple-element.30), channel_id=1, source_target_pairs={{0,7},{1,8},{2,9},{3,10},{4,11},{5,12},{6,13},{7,14},{8,15},{9,16}... | collective-permute-start | bytes 43016 | tf_op jit(solution)/shard_map/ppermute | solution.py:63
  498.7 21.0 %collective-permute-start.51 = (f32[3584]{0:T(1024)S(1)}, f32[3584]{0:T(1024)S(1)}, u32[]{:S(2)}, u32[]{:S(2)}) collective-permute-start(f32[3584]{0:T(1024)S(1)} %get-tuple-element.31), channel_id=1, source_target_pairs={{0,6},{1,7},{2,8},{3,9},{4,10},{5,11},{6,12},{7,13},{8,14},{9,15},... | collective-permute-start | bytes 43016 | tf_op jit(solution)/shard_map/ppermute | solution.py:63
  505.9 16.2 %collective-permute-start.50 = (f32[3584]{0:T(1024)S(1)}, f32[3584]{0:T(1024)S(1)}, u32[]{:S(2)}, u32[]{:S(2)}) collective-permute-start(f32[3584]{0:T(1024)S(1)} %get-tuple-element.32), channel_id=1, source_target_pairs={{0,5},{1,6},{2,7},{3,8},{4,9},{5,10},{6,11},{7,12},{8,13},{9,14},{... | collective-permute-start | bytes 43016 | tf_op jit(solution)/shard_map/ppermute | solution.py:63
  508.3 15.8 %collective-permute-start.49 = (f32[3584]{0:T(1024)S(1)}, f32[3584]{0:T(1024)S(1)}, u32[]{:S(2)}, u32[]{:S(2)}) collective-permute-start(f32[3584]{0:T(1024)S(1)} %get-tuple-element.33), channel_id=1, source_target_pairs={{0,4},{1,5},{2,6},{3,7},{4,8},{5,9},{6,10},{7,11},{8,12},{9,13},{1... | collective-permute-start | bytes 43016 | tf_op jit(solution)/shard_map/ppermute | solution.py:63
  512.5 17.3 %collective-permute-start.48 = (f32[3584]{0:T(1024)S(1)}, f32[3584]{0:T(1024)S(1)}, u32[]{:S(2)}, u32[]{:S(2)}) collective-permute-start(f32[3584]{0:T(1024)S(1)} %get-tuple-element.34), channel_id=1, source_target_pairs={{0,3},{1,4},{2,5},{3,6},{4,7},{5,8},{6,9},{7,10},{8,11},{9,12},{10... | collective-permute-start | bytes 43016 | tf_op jit(solution)/shard_map/ppermute | solution.py:63
  515.6 19.1 %collective-permute-start.47 = (f32[3584]{0:T(1024)S(1)}, f32[3584]{0:T(1024)S(1)}, u32[]{:S(2)}, u32[]{:S(2)}) collective-permute-start(f32[3584]{0:T(1024)S(1)} %get-tuple-element.35), channel_id=1, source_target_pairs={{0,2},{1,3},{2,4},{3,5},{4,6},{5,7},{6,8},{7,9},{8,10},{9,11},{10,... | collective-permute-start | bytes 43016 | tf_op jit(solution)/shard_map/ppermute | solution.py:63
  519.6 18.6 %collective-permute-start.46 = (f32[3584]{0:T(1024)S(1)}, f32[3584]{0:T(1024)S(1)}, u32[]{:S(2)}, u32[]{:S(2)}) collective-permute-start(f32[3584]{0:T(1024)S(1)} %get-tuple-element.36), channel_id=1, source_target_pairs={{0,1},{1,2},{2,3},{3,4},{4,5},{5,6},{6,7},{7,8},{8,9},{9,10},{10,1... | collective-permute-start | bytes 43016 | tf_op jit(solution)/shard_map/ppermute | solution.py:63
  522.2 19.9 %collective-permute-start.76 = (f32[3584]{0:T(1024)S(1)}, f32[3584]{0:T(1024)S(1)}, u32[]{:S(2)}, u32[]{:S(2)}) collective-permute-start(f32[3584]{0:T(1024)S(1)} %get-tuple-element.6), channel_id=1, source_target_pairs={{0,31},{1,0},{2,1},{3,2},{4,3},{5,4},{6,5},{7,6},{8,7},{9,8},{10,9... | collective-permute-start | bytes 43016 | tf_op jit(solution)/shard_map/ppermute | solution.py:63
  524.1 20.7 %collective-permute-start.75 = (f32[3584]{0:T(1024)S(1)}, f32[3584]{0:T(1024)S(1)}, u32[]{:S(2)}, u32[]{:S(2)}) collective-permute-start(f32[3584]{0:T(1024)S(1)} %get-tuple-element.7), channel_id=1, source_target_pairs={{0,30},{1,31},{2,0},{3,1},{4,2},{5,3},{6,4},{7,5},{8,6},{9,7},{10,... | collective-permute-start | bytes 43016 | tf_op jit(solution)/shard_map/ppermute | solution.py:63
  529.8 17.1 %collective-permute-start.74 = (f32[3584]{0:T(1024)S(1)}, f32[3584]{0:T(1024)S(1)}, u32[]{:S(2)}, u32[]{:S(2)}) collective-permute-start(f32[3584]{0:T(1024)S(1)} %get-tuple-element.8), channel_id=1, source_target_pairs={{0,29},{1,30},{2,31},{3,0},{4,1},{5,2},{6,3},{7,4},{8,5},{9,6},{10... | collective-permute-start | bytes 43016 | tf_op jit(solution)/shard_map/ppermute | solution.py:63
  534.7 16.2 %collective-permute-start.73 = (f32[3584]{0:T(1024)S(1)}, f32[3584]{0:T(1024)S(1)}, u32[]{:S(2)}, u32[]{:S(2)}) collective-permute-start(f32[3584]{0:T(1024)S(1)} %get-tuple-element.9), channel_id=1, source_target_pairs={{0,28},{1,29},{2,30},{3,31},{4,0},{5,1},{6,2},{7,3},{8,4},{9,5},{1... | collective-permute-start | bytes 43016 | tf_op jit(solution)/shard_map/ppermute | solution.py:63
  538.3 15.4 %collective-permute-start.72 = (f32[3584]{0:T(1024)S(1)}, f32[3584]{0:T(1024)S(1)}, u32[]{:S(2)}, u32[]{:S(2)}) collective-permute-start(f32[3584]{0:T(1024)S(1)} %get-tuple-element.10), channel_id=1, source_target_pairs={{0,27},{1,28},{2,29},{3,30},{4,31},{5,0},{6,1},{7,2},{8,3},{9,4},{... | collective-permute-start | bytes 43016 | tf_op jit(solution)/shard_map/ppermute | solution.py:63
  542.1 15.6 %collective-permute-start.71 = (f32[3584]{0:T(1024)S(1)}, f32[3584]{0:T(1024)S(1)}, u32[]{:S(2)}, u32[]{:S(2)}) collective-permute-start(f32[3584]{0:T(1024)S(1)} %get-tuple-element.11), channel_id=1, source_target_pairs={{0,26},{1,27},{2,28},{3,29},{4,30},{5,31},{6,0},{7,1},{8,2},{9,3},... | collective-permute-start | bytes 43016 | tf_op jit(solution)/shard_map/ppermute | solution.py:63
  544.8 17.6 %collective-permute-start.70 = (f32[3584]{0:T(1024)S(1)}, f32[3584]{0:T(1024)S(1)}, u32[]{:S(2)}, u32[]{:S(2)}) collective-permute-start(f32[3584]{0:T(1024)S(1)} %get-tuple-element.12), channel_id=1, source_target_pairs={{0,25},{1,26},{2,27},{3,28},{4,29},{5,30},{6,31},{7,0},{8,1},{9,2}... | collective-permute-start | bytes 43016 | tf_op jit(solution)/shard_map/ppermute | solution.py:63
  546.9 20.3 %collective-permute-start.69 = (f32[3584]{0:T(1024)S(1)}, f32[3584]{0:T(1024)S(1)}, u32[]{:S(2)}, u32[]{:S(2)}) collective-permute-start(f32[3584]{0:T(1024)S(1)} %get-tuple-element.13), channel_id=1, source_target_pairs={{0,24},{1,25},{2,26},{3,27},{4,28},{5,29},{6,30},{7,31},{8,0},{9,1... | collective-permute-start | bytes 43016 | tf_op jit(solution)/shard_map/ppermute | solution.py:63
  551.0 19.8 %collective-permute-start.68 = (f32[3584]{0:T(1024)S(1)}, f32[3584]{0:T(1024)S(1)}, u32[]{:S(2)}, u32[]{:S(2)}) collective-permute-start(f32[3584]{0:T(1024)S(1)} %get-tuple-element.14), channel_id=1, source_target_pairs={{0,23},{1,24},{2,25},{3,26},{4,27},{5,28},{6,29},{7,30},{8,31},{9,... | collective-permute-start | bytes 43016 | tf_op jit(solution)/shard_map/ppermute | solution.py:63
  553.7 22.3 %collective-permute-start.67 = (f32[3584]{0:T(1024)}, f32[3584]{0:T(1024)}, u32[]{:S(2)}, u32[]{:S(2)}) collective-permute-start(f32[3584]{0:T(1024)} %get-tuple-element.15), channel_id=1, source_target_pairs={{0,22},{1,23},{2,24},{3,25},{4,26},{5,27},{6,28},{7,29},{8,30},{9,... | collective-permute-start | bytes 43016 | tf_op jit(solution)/shard_map/ppermute | solution.py:63
  557.7 22.8 %collective-permute-start.66 = (f32[3584]{0:T(1024)}, f32[3584]{0:T(1024)}, u32[]{:S(2)}, u32[]{:S(2)}) collective-permute-start(f32[3584]{0:T(1024)} %get-tuple-element.16), channel_id=1, source_target_pairs={{0,21},{1,22},{2,23},{3,24},{4,25},{5,26},{6,27},{7,28},{8,29},{9,... | collective-permute-start | bytes 43016 | tf_op jit(solution)/shard_map/ppermute | solution.py:63
  562.4 20.7 %collective-permute-start.65 = (f32[3584]{0:T(1024)S(1)}, f32[3584]{0:T(1024)}, u32[]{:S(2)}, u32[]{:S(2)}) collective-permute-start(f32[3584]{0:T(1024)S(1)} %get-tuple-element.17), channel_id=1, source_target_pairs={{0,20},{1,21},{2,22},{3,23},{4,24},{5,25},{6,26},{7,27},{8,28},{9,... | collective-permute-start | bytes 43016 | tf_op jit(solution)/shard_map/ppermute | solution.py:63
  567.3 19.5 %collective-permute-start.64 = (f32[3584]{0:T(1024)S(1)}, f32[3584]{0:T(1024)}, u32[]{:S(2)}, u32[]{:S(2)}) collective-permute-start(f32[3584]{0:T(1024)S(1)} %get-tuple-element.18), channel_id=1, source_target_pairs={{0,19},{1,20},{2,21},{3,22},{4,23},{5,24},{6,25},{7,26},{8,27},{9,... | collective-permute-start | bytes 43016 | tf_op jit(solution)/shard_map/ppermute | solution.py:63
  570.8 20.5 %collective-permute-start.63 = (f32[3584]{0:T(1024)S(1)}, f32[3584]{0:T(1024)}, u32[]{:S(2)}, u32[]{:S(2)}) collective-permute-start(f32[3584]{0:T(1024)S(1)} %get-tuple-element.19), channel_id=1, source_target_pairs={{0,18},{1,19},{2,20},{3,21},{4,22},{5,23},{6,24},{7,25},{8,26},{9,... | collective-permute-start | bytes 43016 | tf_op jit(solution)/shard_map/ppermute | solution.py:63
  576.0 24.7 %collective-permute-start.62 = (f32[3584]{0:T(1024)S(1)}, f32[3584]{0:T(1024)S(1)}, u32[]{:S(2)}, u32[]{:S(2)}) collective-permute-start(f32[3584]{0:T(1024)S(1)} %get-tuple-element.20), channel_id=1, source_target_pairs={{0,17},{1,18},{2,19},{3,20},{4,21},{5,22},{6,23},{7,24},{8,25},{9,... | collective-permute-start | bytes 43016 | tf_op jit(solution)/shard_map/ppermute | solution.py:63
  580.5 20.2 %collective-permute-start.61 = (f32[3584]{0:T(1024)S(1)}, f32[3584]{0:T(1024)S(1)}, u32[]{:S(2)}, u32[]{:S(2)}) collective-permute-start(f32[3584]{0:T(1024)S(1)} %get-tuple-element.21), channel_id=1, source_target_pairs={{0,16},{1,17},{2,18},{3,19},{4,20},{5,21},{6,22},{7,23},{8,24},{9,... | collective-permute-start | bytes 43016 | tf_op jit(solution)/shard_map/ppermute | solution.py:63
  583.1 17.6 %collective-permute-start.60 = (f32[3584]{0:T(1024)S(1)}, f32[3584]{0:T(1024)S(1)}, u32[]{:S(2)}, u32[]{:S(2)}) collective-permute-start(f32[3584]{0:T(1024)S(1)} %get-tuple-element.22), channel_id=1, source_target_pairs={{0,15},{1,16},{2,17},{3,18},{4,19},{5,20},{6,21},{7,22},{8,23},{9,... | collective-permute-start | bytes 43016 | tf_op jit(solution)/shard_map/ppermute | solution.py:63
  586.7 14.1 %collective-permute-start.59 = (f32[3584]{0:T(1024)S(1)}, f32[3584]{0:T(1024)S(1)}, u32[]{:S(2)}, u32[]{:S(2)}) collective-permute-start(f32[3584]{0:T(1024)S(1)} %get-tuple-element.23), channel_id=1, source_target_pairs={{0,14},{1,15},{2,16},{3,17},{4,18},{5,19},{6,20},{7,21},{8,22},{9,... | collective-permute-start | bytes 43016 | tf_op jit(solution)/shard_map/ppermute | solution.py:63
  591.3 9.5 %collective-permute-start.58 = (f32[3584]{0:T(1024)S(1)}, f32[3584]{0:T(1024)S(1)}, u32[]{:S(2)}, u32[]{:S(2)}) collective-permute-start(f32[3584]{0:T(1024)S(1)} %get-tuple-element.24), channel_id=1, source_target_pairs={{0,13},{1,14},{2,15},{3,16},{4,17},{5,18},{6,19},{7,20},{8,21},{9,... | collective-permute-start | bytes 43016 | tf_op jit(solution)/shard_map/ppermute | solution.py:63
  609.2 19.7 %collective-permute-start.77 = (bf16[2,5120]{1,0:T(2,128)(2,1)S(1)}, bf16[2,5120]{1,0:T(2,128)(2,1)S(1)}, u32[]{:S(2)}, u32[]{:S(2)}) collective-permute-start(bf16[2,5120]{1,0:T(2,128)(2,1)S(1)} %get-tuple-element.69), channel_id=1, source_target_pairs={{0,1},{1,2},{2,3},{3,4},{4,5},{5,6},{6,7},{7,8},{8,9},{9,10},{10,1... | collective-permute-start | bytes 61448 | tf_op jit(solution)/shard_map/ppermute | solution.py:63
  612.4 216.7 %collective-permute-start.107 = (bf16[2,5120]{1,0:T(2,128)(2,1)S(1)}, bf16[2,5120]{1,0:T(2,128)(2,1)S(1)}, u32[]{:S(2)}, u32[]{:S(2)}) collective-permute-start(bf16[2,5120]{1,0:T(2,128)(2,1)S(1)} %get-tuple-element.39), channel_id=1, source_target_pairs={{0,31},{1,0},{2,1},{3,2},{4,3},{5,4},{6,5},{7,6},{8,7},{9,8},{10,9... | collective-permute-start | bytes 61448 | tf_op jit(solution)/shard_map/ppermute | solution.py:63
  614.3 214.7 %collective-permute-start.106 = (bf16[2,5120]{1,0:T(2,128)(2,1)S(1)}, bf16[2,5120]{1,0:T(2,128)(2,1)S(1)}, u32[]{:S(2)}, u32[]{:S(2)}) collective-permute-start(bf16[2,5120]{1,0:T(2,128)(2,1)S(1)} %get-tuple-element.40), channel_id=1, source_target_pairs={{0,30},{1,31},{2,0},{3,1},{4,2},{5,3},{6,4},{7,5},{8,6},{9,7},{10,... | collective-permute-start | bytes 61448 | tf_op jit(solution)/shard_map/ppermute | solution.py:63
  619.7 209.3 %collective-permute-start.105 = (bf16[2,5120]{1,0:T(2,128)(2,1)S(1)}, bf16[2,5120]{1,0:T(2,128)(2,1)S(1)}, u32[]{:S(2)}, u32[]{:S(2)}) collective-permute-start(bf16[2,5120]{1,0:T(2,128)(2,1)S(1)} %get-tuple-element.41), channel_id=1, source_target_pairs={{0,29},{1,30},{2,31},{3,0},{4,1},{5,2},{6,3},{7,4},{8,5},{9,6},{10... | collective-permute-start | bytes 61448 | tf_op jit(solution)/shard_map/ppermute | solution.py:63
  623.3 205.7 %collective-permute-start.104 = (bf16[2,5120]{1,0:T(2,128)(2,1)S(1)}, bf16[2,5120]{1,0:T(2,128)(2,1)S(1)}, u32[]{:S(2)}, u32[]{:S(2)}) collective-permute-start(bf16[2,5120]{1,0:T(2,128)(2,1)S(1)} %get-tuple-element.42), channel_id=1, source_target_pairs={{0,28},{1,29},{2,30},{3,31},{4,0},{5,1},{6,2},{7,3},{8,4},{9,5},{1... | collective-permute-start | bytes 61448 | tf_op jit(solution)/shard_map/ppermute | solution.py:63
  713.1 10.0 %collective-permute-start.89 = (bf16[2,5120]{1,0:T(2,128)(2,1)S(1)}, bf16[2,5120]{1,0:T(2,128)(2,1)S(1)}, u32[]{:S(2)}, u32[]{:S(2)}) collective-permute-start(bf16[2,5120]{1,0:T(2,128)(2,1)S(1)} %get-tuple-element.57), channel_id=1, source_target_pairs={{0,13},{1,14},{2,15},{3,16},{4,17},{5,18},{6,19},{7,20},{8,21},{9,... | collective-permute-start | bytes 61448 | tf_op jit(solution)/shard_map/ppermute | solution.py:63
  774.9 10.6 %collective-permute-start.97 = (bf16[2,5120]{1,0:T(2,128)(2,1)S(1)}, bf16[2,5120]{1,0:T(2,128)(2,1)S(1)}, u32[]{:S(2)}, u32[]{:S(2)}) collective-permute-start(bf16[2,5120]{1,0:T(2,128)(2,1)S(1)} %get-tuple-element.49), channel_id=1, source_target_pairs={{0,21},{1,22},{2,23},{3,24},{4,25},{5,26},{6,27},{7,28},{8,29},{9,... | collective-permute-start | bytes 61448 | tf_op jit(solution)/shard_map/ppermute | solution.py:63
  790.9 11.3 %collective-permute-start.99 = (bf16[2,5120]{1,0:T(2,128)(2,1)S(1)}, bf16[2,5120]{1,0:T(2,128)(2,1)S(1)}, u32[]{:S(2)}, u32[]{:S(2)}) collective-permute-start(bf16[2,5120]{1,0:T(2,128)(2,1)S(1)} %get-tuple-element.47), channel_id=1, source_target_pairs={{0,23},{1,24},{2,25},{3,26},{4,27},{5,28},{6,29},{7,30},{8,31},{9,... | collective-permute-start | bytes 61448 | tf_op jit(solution)/shard_map/ppermute | solution.py:63
  818.6 10.3 %collective-permute-start.103 = (bf16[2,5120]{1,0:T(2,128)(2,1)S(1)}, bf16[2,5120]{1,0:T(2,128)(2,1)S(1)}, u32[]{:S(2)}, u32[]{:S(2)}) collective-permute-start(bf16[2,5120]{1,0:T(2,128)(2,1)S(1)} %get-tuple-element.43), channel_id=1, source_target_pairs={{0,27},{1,28},{2,29},{3,30},{4,31},{5,0},{6,1},{7,2},{8,3},{9,4},{... | collective-permute-start | bytes 61448 | tf_op jit(solution)/shard_map/ppermute | solution.py:63
  (102 other events, 2266.7 us)

commit v3 on v1

--- a/solution.py
+++ b/solution.py
@@ -91,8 +91,10 @@
     down_flat = adapter_down_maps.reshape(1, -1)
     query_flat = adapter_query_up.reshape(1, -1)
     value_flat = adapter_value_up.reshape(1, -1)
-    bank = lax.all_gather(
-        jnp.concatenate([down_flat, query_flat, value_flat], axis=1), "req", axis=0, tiled=True
+    bank_piece = jnp.concatenate([down_flat, query_flat, value_flat], axis=1)
+    req_width = lax.axis_size("req")
+    bank = lax.all_to_all(
+        jnp.broadcast_to(bank_piece, (req_width, bank_piece.shape[1])), "req", 0, 0, tiled=True
     )
     adapter_total = bank.shape[0]
     n_down, n_query = down_flat.shape[1], query_flat.shape[1]

time: 125 us -> 108 us (0.86)
  blocking collectives: 81.2 us -> 42.3 us
  starting transfers between devices: 5.1 us -> 20.9 us
  other arithmetic: 9.57 us -> 13.8 us
  local copies, waits for them, and re-layouts: 15.1 us -> 17.3 us
    all_gather x1 -> x0, blocking collectives: 31.6 us -> none  [shards(): lax.all_gather(jnp.concatenate([down_flat, query_flat, value_flat], axis=...]
    all_to_all x0 -> x1, starting transfers between devices: none -> 15.7 us  [shards(): lax.all_to_all(jnp.broadcast_to(bank_piece, (req_width, bank_piece.shape[...]
    all_gather x1, blocking collectives: 33.2 us -> 26 us  [shards(): gathered = lax.all_gather(hidden, 'tp', axis=0, tiled=True)]
    broadcast_in_dim x0 -> x1, other arithmetic: none -> 2.07 us  [shards(): jnp.broadcast_to(bank_piece, (req_width, bank_piece.shape[1]))]
    dot_general x1, matrix products: 0.36 us -> 1.67 us  [shards(): jnp.dot(normalized_input, query_weight, preferred_element_type=jnp.float32)]
    unnamed x38 -> x44, local copies, waits for them, and re-layouts: 3.37 us -> 4.43 us
  transfers between devices with their start and end apart: 1 -> 2, of which waited for: 1 -> 1; matrix products, arithmetic and copies ran while one was open for 1% -> 12% of each run, Pallas kernels for 0% -> 0%
where the time goes in v3:
time: 108 us; the launch traced here: 107 us
  blocking collectives  42.3 us (39%)
  starting transfers between devices  20.9 us (19%)
  local copies, waits for them, and re-layouts  17.3 us (16%)
  other arithmetic  13.8 us (13%)
  waiting for transfers between devices  8.7 us (8%)
  matrix products  3.8 us (4%)
    all_gather x1, blocking collectives, shards(): gathered = lax.all_gather(hidden, 'tp', axis=0, tiled=True)  26 us
    all_to_all x1, blocking collectives, shards(): lax.all_to_all(block_terms.reshape(tp_width, tok_rows, block_terms.shape[...  16.3 us
    all_to_all x1, starting transfers between devices, shards(): lax.all_to_all(jnp.broadcast_to(bank_piece, (req_width, bank_piece.shape[...  15.7 us
    all_to_all x1, waiting for transfers between devices, shards(): lax.all_to_all(jnp.concatenate([key_send, value_send, latent_send, up_sen...  8.69 us
    select_n x1, other arithmetic, shards(): token_adapter = jnp.take(adapter_choice_list, segment)  5.6 us
    all_to_all x1, starting transfers between devices, shards(): lax.all_to_all(jnp.concatenate([key_send, value_send, latent_send, up_sen...  5.11 us
    unnamed x44, local copies, waits for them, and re-layouts  4.43 us
    all_to_all x2, local copies, waits for them, and re-layouts, shards(): lax.all_to_all(jnp.concatenate([key_send, value_send, latent_send, up_sen...  2.66 us
  transfers between devices with their start and end apart: 2, of which 1 were waited for; matrix products, arithmetic and copies ran while one was open for 12% of the time, Pallas kernels for 0%

profile of v3, /device:TPU:1, one launch (start us, length us, event | category | flops | bytes accessed | tf_op | source)
XLA Modules:
  0.0 107.3 jit_solution(14545950278496186811)
XLA Ops:
  0.0 0.8 copy.133
  0.8 0.8 copy.104
  1.6 0.1 reshape.433
  1.7 0.8 copy.103
  2.5 0.1 reshape.431
  2.6 0.1 maximum_reduce_fusion
  2.7 0.3 broadcast_in_dim.48
  3.0 0.5 broadcast.427
  3.5 2.1 %reduce.5 = bf16[16,7680]{1,0:T(8,128)(2,1)S(1)} reduce(bf16[16,1,7680]{2,1,0:T(2,128)(2,1)S(1)} %broadcast_in_dim.48, bf16[]{:T(256)} %broadcast.427), dimensions={1}, to_apply=%broadcast_in_dim.48.reduce_sub_computation | reduce | bytes 491522 | tf_op jit(solution)/shard_map/broadcast_in_dim | solution.py:97
  5.6 0.7 reshape.552
  6.3 15.7 %all-to-all-start = ((bf16[16,2,3840]{2,1,0:T(2,128)(2,1)}), bf16[16,2,3840]{2,1,0:T(2,128)(2,1)S(1)}, u32[]{:S(2)}, u32[]{:S(2)}) async-start(bf16[16,2,3840]{2,1,0:T(2,128)(2,1)} %reshape.552), calls=%async_computation | async-start | bytes 491520 | tf_op jit(solution)/shard_map/all_to_all | solution.py:96
  22.2 26.0 %all-gather = bf16[32,2,5120]{2,1,0:T(2,128)(2,1)S(1)} all-gather(bf16[1,2,5120]{2,1,0:T(2,128)(2,1)S(1)} %bitcast.143), channel_id=1, replica_groups=mesh['req'=16,'tp'=32] {'tp'}, dimensions={0}, use_global_device_ids=true | all-gather | bytes 675840 | tf_op jit(solution)/shard_map/all_gather | solution.py:113
  48.1 0.2 reshape.532
  48.3 0.2 multiply_reduce_fusion
  48.6 0.3 copy-done.8
  48.9 0.2 multiply_convert_fusion
  49.1 0.4 copy-done.3
  49.5 0.3 fusion.6
  49.9 0.3 convolution_bitcast_fusion.2
  50.2 0.6 gather_fusion.1
  50.8 0.6 gather_fusion.2
  51.4 0.1 broadcast_select_fusion.1
  51.6 0.2 reduce-window.4
  51.8 0.1 copy.100
  51.9 0.1 copy.102
  52.1 0.7 copy.112
  52.7 0.7 fusion.53
  53.4 0.1 select_reduce_fusion.1
  53.5 5.6 %and_select_fusion.1 = (s32[64]{0:T(128)S(1)}, f32[64]{0:T(128)}) fusion(s32[64]{0:T(128)S(1)} %get-tuple-element.7, s32[]{:T(128)} %bitcast.18, s32[]{:T(128)} %bitcast.19, s32[]{:T(128)} %bitcast.20, s32[]{:T(128)} %bitcast.21, s32[]{:T(128)} %bitcast.22, s32[]{:T(128)} %bitcast.24, s32[]{:T(128)} %bitcast.23, s32[]{:T(128)} %bitcast.17, ...), kind=kLoop, calls=%fused_computation.95 | loop fusion | flops 1664 | bytes 1056 | tf_op jit(solution)/shard_map/jit(_take)/select_n | solution.py:110
  59.1 0.6 fusion.50
  59.7 0.2 reshape.553
  60.0 0.7 slice.78
  60.6 0.1 copy.107
  60.8 0.2 copy.108
  61.0 0.7 gather_fusion
  61.7 0.7 copy.109
  62.4 0.7 select_convert_fusion
  63.1 0.2 copy.110
  63.3 0.8 copy.113
  64.1 0.4 reshape.434
  64.5 0.3 copy.105
  64.9 0.3 fusion.29
  65.2 0.7 select_reduce_fusion
  66.1 0.8 pad_maximum_fusion
  66.9 1.1 %all_to_all.19 = f32[32,1,3584]{2,1,0:T(1,128)} reshape(f32[32,3584]{1,0:T(8,128)S(1)} %pad_maximum_fusion) | data formatting | bytes 917504 | tf_op jit(solution)/shard_map/all_to_all | solution.py:145
  68.0 5.1 %all-to-all-start.1 = ((f32[32,1,3584]{2,1,0:T(1,128)}), f32[32,1,3584]{2,1,0:T(1,128)}, u32[]{:S(2)}, u32[]{:S(2)}) async-start(f32[32,1,3584]{2,1,0:T(1,128)} %all_to_all.19), calls=%async_computation.1 | async-start | bytes 917504 | tf_op jit(solution)/shard_map/all_to_all | solution.py:145
  73.1 0.6 multiply_power_fusion
  73.7 1.7 %convolution_add_fusion.1 = f32[64,128]{1,0:T(8,128)S(1)} fusion(bf16[64,5120]{1,0:T(8,128)(2,1)S(1)} %multiply_convert_fusion, bf16[5120,128]{1,0:T(8,128)(2,1)} %param.17, f32[128]{0:T(128)S(1)} %copy-done.15), kind=kOutput, calls=%fused_computation.11 | convolution fusion | flops 83894272 | bytes 1999360 | tf_op jit(solution)/shard_map/dot_general | solution.py:185
  75.4 8.7 %all-to-all-done.1 = f32[32,1,3584]{2,1,0:T(1,128)} async-done(((f32[32,1,3584]{2,1,0:T(1,128)}), f32[32,1,3584]{2,1,0:T(1,128)}, u32[]{:S(2)}, u32[]{:S(2)}) %all-to-all-start.1) | async-done | bytes 458784 | tf_op jit(solution)/shard_map/all_to_all | solution.py:145
  84.1 1.6 %copy.114 = f32[32,1,3584]{0,2,1:T(8,128)S(1)} copy(f32[32,1,3584]{2,1,0:T(1,128)} %all-to-all-done.1) | data formatting | bytes 917504 | tf_op jit(solution)/shard_map/all_to_all | solution.py:145
  85.7 0.3 slice_reduce_fusion
  86.1 0.1 bitcast_convert_fusion
  86.5 0.1 copy.115
  86.7 0.1 copy.120
  87.0 1.0 copy.117
  88.0 0.2 fusion.1
  88.2 0.2 fusion.43
  88.5 0.2 fusion.54
  88.7 0.3 fusion.3
  89.1 0.5 convolution_convert_fusion
  89.6 0.2 reshape.443
  89.9 16.3 %all_to_all.26 = bf16[32,2,5120]{2,1,0:T(2,128)(2,1)S(1)} all-to-all(bf16[32,2,5120]{2,1,0:T(2,128)(2,1)S(1)} %reshape.443), channel_id=1, replica_groups=mesh['req'=16,'tp'=32] {'tp'}, dimensions={0} | all-to-all | bytes 1310720 | tf_op jit(solution)/shard_map/all_to_all | solution.py:214
  106.2 0.5 convert_reduce_fusion
  106.7 0.6 add_convert_fusion
  (65 shorter events, 1.1 us)
Async XLA Ops:
  0.0 89.1 %copy-start = (bf16[128,5120]{1,0:T(8,128)(2,1)S(1)}, bf16[128,5120]{1,0:T(8,128)(2,1)}, u32[]{:S(2)}) copy-start(bf16[128,5120]{1,0:T(8,128)(2,1)} %param.20) | copy-start | bytes 3932164
  0.0 22.2 %copy-start.5 = (bf16[2,5120]{1,0:T(2,128)(2,1)S(1)}, bf16[2,5120]{1,0:T(2,128)(2,1)}, u32[]{:S(2)}) copy-start(bf16[2,5120]{1,0:T(2,128)(2,1)} %param.15) | copy-start | bytes 61444
  6.3 53.4 %all-to-all-start = ((bf16[16,2,3840]{2,1,0:T(2,128)(2,1)}), bf16[16,2,3840]{2,1,0:T(2,128)(2,1)S(1)}, u32[]{:S(2)}, u32[]{:S(2)}) async-start(bf16[16,2,3840]{2,1,0:T(2,128)(2,1)} %reshape.552), calls=%async_computation | async-start | bytes 491520 | tf_op jit(solution)/shard_map/all_to_all | solution.py:96
  22.1 29.3 %copy-start.14 = (pred[32]{0:T(512)(128)(4,1)}, pred[32]{0:T(512)(128)(4,1)S(1)}, u32[]{:S(2)}) copy-start(pred[32]{0:T(512)(128)(4,1)S(1)} %compare_and_fusion) | copy-start | bytes 100
  48.1 0.7 copy-start.8
  48.5 1.0 copy-start.3
  48.5 1.0 copy-start.10
  48.9 1.0 copy-start.4
  50.8 0.8 copy-start.17
  50.8 1.9 %copy-start.7 = (s32[1,8]{1,0:T(1,128)S(1)}, s32[1,8]{1,0:T(1,128)}, u32[]{:S(2)}) copy-start(s32[1,8]{1,0:T(1,128)} %param.27) | copy-start | bytes 100
  53.5 8.2 %copy-start.12 = (s32[64]{0:T(128)}, s32[64]{0:T(128)S(1)}, u32[]{:S(2)}) copy-start(s32[64]{0:T(128)S(1)} %get-tuple-element.7) | copy-start | bytes 772
  63.0 1.0 copy-start.1
  64.5 1.5 %copy-start.2 = (f32[32,1024]{1,0:T(8,128)S(1)}, f32[32,1024]{1,0:T(8,128)}, u32[]{:S(2)}) copy-start(f32[32,1024]{1,0:T(8,128)} %copy.113) | copy-start | bytes 393220
  65.9 7.8 %copy-start.15 = (f32[128]{0:T(128)S(1)}, f32[128]{0:T(128)}, u32[]{:S(2)}) copy-start(f32[128]{0:T(128)} %param.21) | copy-start | bytes 1540
  68.0 16.1 %all-to-all-start.1 = ((f32[32,1,3584]{2,1,0:T(1,128)}), f32[32,1,3584]{2,1,0:T(1,128)}, u32[]{:S(2)}, u32[]{:S(2)}) async-start(f32[32,1,3584]{2,1,0:T(1,128)} %all_to_all.19), calls=%async_computation.1 | async-start | bytes 917504 | tf_op jit(solution)/shard_map/all_to_all | solution.py:145
  86.2 1.9 %copy-start.9 = (bf16[64,16]{0,1:T(8,128)(2,1)S(1)}, bf16[64,16]{0,1:T(8,128)(2,1)}, u32[]{:S(2)}) copy-start(bf16[64,16]{0,1:T(8,128)(2,1)} %get-tuple-element.18) | copy-start | bytes 6148
  86.2 2.1 %copy-start.11 = (f32[64]{0:T(128)S(1)}, f32[64]{0:T(128)}, u32[]{:S(2)}) copy-start(f32[64]{0:T(128)} %get-tuple-element.33) | copy-start | bytes 772
  86.2 2.1 %copy-start.16 = (f32[64]{0:T(128)S(1)}, f32[64]{0:T(128)}, u32[]{:S(2)}) copy-start(f32[64]{0:T(128)} %multiply_power_fusion) | copy-start | bytes 772
  86.2 2.2 %copy-start.13 = (s32[64]{0:T(128)S(1)}, s32[64]{0:T(128)}, u32[]{:S(2)}) copy-start(s32[64]{0:T(128)} %copy-done.12) | copy-start | bytes 772
  89.8 16.9 %copy-start.6 = (bf16[2,5120]{1,0:T(2,128)(2,1)S(1)}, bf16[2,5120]{1,0:T(2,128)(2,1)}, u32[]{:S(2)}) copy-start(bf16[2,5120]{1,0:T(2,128)(2,1)} %param.15) | copy-start | bytes 61444

commit v4 on v3

--- a/solution.py
+++ b/solution.py
@@ -13,15 +13,16 @@
 
 
 def prompt_layout(prompt_length_list, group_tokens):
-    ends = jnp.cumsum(prompt_length_list)
+    count = prompt_length_list.shape[0]
+    prompts = jnp.arange(count, dtype=jnp.int32)
+    ends = jnp.sum(
+        jnp.where(prompts[None, :] <= prompts[:, None], prompt_length_list[None, :], 0), axis=1
+    )
     starts = ends - prompt_length_list
     places = jnp.arange(group_tokens, dtype=jnp.int32)
     group_entry = (places[:, None] >= starts[None, :]) & (places[:, None] < ends[None, :])
-    chosen = group_entry.astype(jnp.int32)
-    segment = jnp.sum(
-        chosen * jnp.arange(prompt_length_list.shape[0], dtype=jnp.int32)[None, :], axis=1
-    )
-    offset = places - jnp.sum(chosen * starts[None, :], axis=1)
+    segment = jnp.sum(jnp.where(group_entry, prompts[None, :], 0), axis=1)
+    offset = places - jnp.sum(jnp.where(group_entry, starts[None, :], 0), axis=1)
     return (group_entry, segment, offset)
 
 
@@ -93,9 +94,7 @@
     value_flat = adapter_value_up.reshape(1, -1)
     bank_piece = jnp.concatenate([down_flat, query_flat, value_flat], axis=1)
     req_width = lax.axis_size("req")
-    bank = lax.all_to_all(
-        jnp.broadcast_to(bank_piece, (req_width, bank_piece.shape[1])), "req", 0, 0, tiled=True
-    )
+    bank = lax.all_to_all(jnp.tile(bank_piece, (req_width, 1)), "req", 0, 0, tiled=True)
     adapter_total = bank.shape[0]
     n_down, n_query = down_flat.shape[1], query_flat.shape[1]
     bank_down = bank[:, :n_down].reshape((adapter_total,) + adapter_down_maps.shape[1:])
@@ -107,7 +106,7 @@
     prompt_length_list = lengths[0]
     adapter_choice_list = prompt_adapter[0]
     group_entry, segment, offset = prompt_layout(prompt_length_list, group_tokens)
-    token_adapter = jnp.take(adapter_choice_list, segment)
+    token_adapter = jnp.sum(jnp.where(group_entry, adapter_choice_list[None, :], 0), axis=1)
     adapter_pick = token_adapter[:, None] == jnp.arange(adapter_total, dtype=jnp.int32)[None, :]
 
     gathered = lax.all_gather(hidden, "tp", axis=0, tiled=True)
@@ -116,9 +115,11 @@
     own_features = lax.dynamic_slice_in_dim(
         normalized_input, tp_place * feat_slice, feat_slice, 1
     )
-    terms = jnp.einsum(
-        "tf,afr->tar", own_features, bank_down, preferred_element_type=jnp.float32
-    )
+    terms = jnp.dot(
+        own_features,
+        jnp.transpose(bank_down, (1, 0, 2)).reshape(feat_slice, -1),
+        preferred_element_type=jnp.float32,
+    ).reshape(group_tokens, adapter_total, 2 * rank_extent)
     latent_part = jnp.sum(jnp.where(adapter_pick[:, :, None], terms, 0.0), axis=1)
 
     key_cols = jnp.einsum(
@@ -130,16 +131,12 @@
         )
         + jnp.transpose(value_bias_vector)[None, :, :]
     )
-    dest = jnp.arange(tp_width, dtype=jnp.int32)
-    dest_head = dest * head_count // (HQ // HK)
-    key_send = jnp.take(key_cols, dest_head, axis=1).transpose(1, 0, 2).reshape(tp_width, -1)
-    value_send = jnp.take(value_cols, dest_head, axis=1).transpose(1, 0, 2).reshape(tp_width, -1)
+    per_kv = tp_width // kv_heads
+    key_send = jnp.repeat(key_cols.transpose(1, 0, 2), per_kv, axis=0).reshape(tp_width, -1)
+    value_send = jnp.repeat(value_cols.transpose(1, 0, 2), per_kv, axis=0).reshape(tp_width, -1)
     latent_send = jnp.broadcast_to(latent_part.reshape(1, -1), (tp_width, latent_part.size))
-    up_send = (
-        jnp.take(bank_value, dest_head, axis=3)
-        .astype(jnp.float32)
-        .transpose(3, 0, 1, 2)
-        .reshape(tp_width, -1)
+    up_send = jnp.repeat(
+        bank_value.transpose(3, 0, 1, 2).reshape(kv_heads, -1).astype(jnp.float32), per_kv, axis=0
     )
     n_key, n_value, n_latent = key_send.shape[1], value_send.shape[1], latent_send.shape[1]
     received = lax.all_to_all(

time: 108 us -> 105 us (0.972)
  other arithmetic: 13.8 us -> 7.85 us
  local copies, waits for them, and re-layouts: 17.3 us -> 19.2 us
    select_n x4 -> x0, other arithmetic: 5.71 us -> none  [the longest x1 5.6 us: shards(): token_adapter = jnp.take(adapter_choice_list, segment)]
    another operation x0 -> x4, local copies, waits for them, and re-layouts: none -> 3.29 us  [the longest x1 1.26 us: shards(): jnp.repeat(key_cols.transpose(1, 0, 2), per_kv, axis=0)]
    gather x5 -> x0, local copies, waits for them, and re-layouts: 3.25 us -> none  [the longest x2 1.36 us: shards(): jnp.take(bank_value, dest_head, axis=3).astype(jnp.float32)]
    broadcast_in_dim x1 -> x0, other arithmetic: 2.07 us -> none  [shards(): jnp.broadcast_to(bank_piece, (req_width, bank_piece.shape[1]))]
    another operation x2, other arithmetic: 0.27 us -> 2.16 us  [the longest x1 2.07 us: shards(): jnp.tile(bank_piece, (req_width, 1))]
    unnamed x44 -> x38, local copies, waits for them, and re-layouts: 4.43 us -> 5.79 us
    reshape x5 -> x1, local copies, waits for them, and re-layouts: 1.99 us -> 0.68 us  [shards(): jnp.repeat(bank_value.transpose(3, 0, 1, 2).reshape(kv_heads, -1).astype(...]
  transfers between devices with their start and end apart: 2 -> 2, of which waited for: 1 -> 1; matrix products, arithmetic and copies ran while one was open for 12% -> 7% of each run, Pallas kernels for 0% -> 0%
where the time goes in v4:
time: 105 us; the launch traced here: 104 us
  blocking collectives  42.3 us (40%)
  starting transfers between devices  20.9 us (20%)
  local copies, waits for them, and re-layouts  19.2 us (18%)
  waiting for transfers between devices  9.41 us (9%)
  other arithmetic  7.85 us (7%)
  matrix products  3.77 us (4%)
    all_gather x1, blocking collectives, shards(): gathered = lax.all_gather(hidden, 'tp', axis=0, tiled=True)  26 us
    all_to_all x1, blocking collectives, shards(): lax.all_to_all(block_terms.reshape(tp_width, tok_rows, block_terms.shape[...  16.3 us
    all_to_all x1, starting transfers between devices, shards(): lax.all_to_all(jnp.tile(bank_piece, (req_width, 1)), 'req', 0, 0, tiled=T...  15.8 us
    all_to_all x1, waiting for transfers between devices, shards(): lax.all_to_all(jnp.concatenate([key_send, value_send, latent_send, up_sen...  9.41 us
    unnamed x38, local copies, waits for them, and re-layouts  5.79 us
    all_to_all x1, starting transfers between devices, shards(): lax.all_to_all(jnp.concatenate([key_send, value_send, latent_send, up_sen...  5.13 us
    all_to_all x2, local copies, waits for them, and re-layouts, shards(): lax.all_to_all(jnp.concatenate([key_send, value_send, latent_send, up_sen...  2.66 us
  transfers between devices with their start and end apart: 2, of which 1 were waited for; matrix products, arithmetic and copies ran while one was open for 7% of the time, Pallas kernels for 0%

profile of v4, /device:TPU:1, one launch (start us, length us, event | category | flops | bytes accessed | tf_op | source)
XLA Modules:
  0.0 103.9 jit_solution(11695515793631954779)
XLA Ops:
  0.0 0.8 copy.99
  0.8 0.8 copy.74
  1.6 0.1 reshape.344
  1.7 0.8 copy.73
  2.5 0.1 reshape.342
  2.6 0.1 maximum_reduce_fusion
  2.7 0.3 tile.2
  3.0 0.5 broadcast.199
  3.5 2.1 %reduce.5 = bf16[16,7680]{1,0:T(8,128)(2,1)S(1)} reduce(bf16[16,1,7680]{2,1,0:T(2,128)(2,1)S(1)} %tile.2, bf16[]{:T(256)} %broadcast.199), dimensions={1}, to_apply=%tile.2.reduce_sub_computation | reduce | bytes 491522 | tf_op jit(solution)/shard_map/tile | solution.py:97
  5.6 0.7 reshape.366
  6.3 15.8 %all-to-all-start = ((bf16[16,2,3840]{2,1,0:T(2,128)(2,1)}), bf16[16,2,3840]{2,1,0:T(2,128)(2,1)}, u32[]{:S(2)}, u32[]{:S(2)}) async-start(bf16[16,2,3840]{2,1,0:T(2,128)(2,1)} %reshape.366), calls=%async_computation | async-start | bytes 491520 | tf_op jit(solution)/shard_map/all_to_all | solution.py:97
  22.2 26.0 %all-gather = bf16[32,2,5120]{2,1,0:T(2,128)(2,1)S(1)} all-gather(bf16[1,2,5120]{2,1,0:T(2,128)(2,1)S(1)} %bitcast.122), channel_id=1, replica_groups=mesh['req'=16,'tp'=32] {'tp'}, dimensions={0}, use_global_device_ids=true | all-gather | bytes 675840 | tf_op jit(solution)/shard_map/all_gather | solution.py:112
  48.1 0.2 reshape.360
  48.3 0.2 multiply_reduce_fusion
  48.5 0.3 copy-done.6
  48.9 0.2 multiply_convert_fusion
  49.1 0.4 copy-done.2
  49.5 0.3 convolution_bitcast_fusion.2
  49.8 0.2 copy.71
  50.0 0.5 copy-done.3
  50.5 0.3 fusion.7
  50.8 0.2 copy.72
  50.9 0.1 broadcast_in_dim.65
  51.1 1.3 %reshape_reshape.10 = f32[32,256]{1,0:T(8,128)} reshape(f32[8,4,64,4]{3,2,1,0:T(8,128)S(1)} %broadcast_in_dim.65) | data formatting | bytes 65536 | tf_op jit(solution)/shard_map/reshape;reshape | solution.py:136
  52.3 0.1 broadcast_in_dim.64
  52.4 1.3 %reshape_reshape.9 = f32[32,256]{1,0:T(8,128)} reshape(f32[8,4,64,4]{3,2,1,0:T(8,128)S(1)} %broadcast_in_dim.64) | data formatting | bytes 65536 | tf_op jit(solution)/shard_map/reshape;reshape | solution.py:135
  53.7 0.6 multiply_power_fusion
  54.3 0.1 select_reduce_fusion.3
  54.4 0.7 select_reduce_fusion.1
  55.1 0.6 fusion.50
  55.7 1.1 %reshape.367 = bf16[16,1,7680]{2,1,0:T(2,128)(2,1)S(1)} reshape(bf16[16,2,3840]{2,1,0:T(2,128)(2,1)} %all-to-all-done) | data formatting | bytes 491520
  56.9 0.1 copy.77
  57.0 0.6 copy.78
  57.6 0.2 copy.79
  57.8 0.7 reshape.347
  58.5 0.4 reshape.345
  58.9 0.3 copy.75
  59.3 0.9 fusion
  60.2 0.9 copy.76
  61.1 0.7 reshape.365
  61.8 0.7 pad.6.clone
  62.5 0.9 pad_maximum_fusion
  63.4 1.1 %all_to_all.19 = f32[32,1,3584]{2,1,0:T(1,128)} reshape(f32[32,3584]{1,0:T(8,128)S(1)} %pad_maximum_fusion) | data formatting | bytes 917504 | tf_op jit(solution)/shard_map/all_to_all | solution.py:142
  64.5 5.1 %all-to-all-start.1 = ((f32[32,1,3584]{2,1,0:T(1,128)}), f32[32,1,3584]{2,1,0:T(1,128)}, u32[]{:S(2)}, u32[]{:S(2)}) async-start(f32[32,1,3584]{2,1,0:T(1,128)} %all_to_all.19), calls=%async_computation.1 | async-start | bytes 917504 | tf_op jit(solution)/shard_map/all_to_all | solution.py:142
  69.7 0.5 subtract_convert_fusion
  70.2 1.0 convolution_add_fusion.1
  71.2 9.4 %all-to-all-done.1 = f32[32,1,3584]{2,1,0:T(1,128)} async-done(((f32[32,1,3584]{2,1,0:T(1,128)}), f32[32,1,3584]{2,1,0:T(1,128)}, u32[]{:S(2)}, u32[]{:S(2)}) %all-to-all-start.1) | async-done | bytes 458784 | tf_op jit(solution)/shard_map/all_to_all | solution.py:142
  80.7 1.6 %copy.80 = f32[32,1,3584]{0,2,1:T(8,128)S(1)} copy(f32[32,1,3584]{2,1,0:T(1,128)} %all-to-all-done.1) | data formatting | bytes 917504 | tf_op jit(solution)/shard_map/all_to_all | solution.py:142
  82.2 0.3 slice_reduce_fusion
  82.6 0.1 bitcast_convert_fusion
  82.8 0.1 convert_element_type.122
  83.1 0.1 copy.81
  83.3 0.1 copy.86
  83.5 0.1 copy.91
  83.6 1.0 copy.83
  84.6 0.2 fusion.2
  84.8 0.2 fusion.45
  85.0 0.2 fusion.53
  85.3 0.3 fusion.4
  85.6 0.5 convolution_convert_fusion
  86.1 0.2 reshape.353
  86.4 16.3 %all_to_all.26 = bf16[32,2,5120]{2,1,0:T(2,128)(2,1)S(1)} all-to-all(bf16[32,2,5120]{2,1,0:T(2,128)(2,1)S(1)} %reshape.353), channel_id=1, replica_groups=mesh['req'=16,'tp'=32] {'tp'}, dimensions={0} | all-to-all | bytes 1310720 | tf_op jit(solution)/shard_map/all_to_all | solution.py:211
  102.7 0.5 convert_reduce_fusion
  103.3 0.6 add_convert_fusion
  (47 shorter events, 0.7 us)
Async XLA Ops:
  0.0 85.6 %copy-start = (bf16[128,5120]{1,0:T(8,128)(2,1)S(1)}, bf16[128,5120]{1,0:T(8,128)(2,1)}, u32[]{:S(2)}) copy-start(bf16[128,5120]{1,0:T(8,128)(2,1)} %param.18) | copy-start | bytes 3932164
  0.0 22.1 %copy-start.4 = (bf16[2,5120]{1,0:T(2,128)(2,1)S(1)}, bf16[2,5120]{1,0:T(2,128)(2,1)}, u32[]{:S(2)}) copy-start(bf16[2,5120]{1,0:T(2,128)(2,1)} %param.13) | copy-start | bytes 61444
  6.3 49.3 %all-to-all-start = ((bf16[16,2,3840]{2,1,0:T(2,128)(2,1)}), bf16[16,2,3840]{2,1,0:T(2,128)(2,1)}, u32[]{:S(2)}, u32[]{:S(2)}) async-start(bf16[16,2,3840]{2,1,0:T(2,128)(2,1)} %reshape.366), calls=%async_computation | async-start | bytes 491520 | tf_op jit(solution)/shard_map/all_to_all | solution.py:97
  48.1 0.7 copy-start.6
  48.5 1.0 copy-start.2
  48.9 1.1 %copy-start.8 = (f32[4,8]{1,0:T(4,128)S(1)}, f32[4,8]{1,0:T(4,128)}, u32[]{:S(2)}) copy-start(f32[4,8]{1,0:T(4,128)} %param.20) | copy-start | bytes 388
  49.5 1.0 copy-start.3
  52.3 2.0 %copy-start.14 = (s32[1,8]{1,0:T(1,128)S(1)}, s32[1,8]{1,0:T(1,128)}, u32[]{:S(2)}) copy-start(s32[1,8]{1,0:T(1,128)} %param.24) | copy-start | bytes 100
  52.3 2.1 %copy-start.11 = (s32[1,8]{1,0:T(1,128)S(1)}, s32[1,8]{1,0:T(1,128)}, u32[]{:S(2)}) copy-start(s32[1,8]{1,0:T(1,128)} %param.25) | copy-start | bytes 100
  60.2 10.0 %copy-start.1 = (bf16[5120,128]{1,0:T(8,128)(2,1)S(1)}, bf16[5120,128]{1,0:T(8,128)(2,1)}, u32[]{:S(2)}) copy-start(bf16[5120,128]{1,0:T(8,128)(2,1)} %param.15) | copy-start | bytes 3932164
  61.8 7.9 %copy-start.13 = (s32[64]{0:T(128)S(1)}, s32[64]{0:T(128)}, u32[]{:S(2)}) copy-start(s32[64]{0:T(128)} %get-tuple-element.6) | copy-start | bytes 772
  64.5 16.1 %all-to-all-start.1 = ((f32[32,1,3584]{2,1,0:T(1,128)}), f32[32,1,3584]{2,1,0:T(1,128)}, u32[]{:S(2)}, u32[]{:S(2)}) async-start(f32[32,1,3584]{2,1,0:T(1,128)} %all_to_all.19), calls=%async_computation.1 | async-start | bytes 917504 | tf_op jit(solution)/shard_map/all_to_all | solution.py:142
  82.7 1.9 %copy-start.7 = (bf16[64,16]{0,1:T(8,128)(2,1)S(1)}, bf16[64,16]{0,1:T(8,128)(2,1)}, u32[]{:S(2)}) copy-start(bf16[64,16]{0,1:T(8,128)(2,1)} %get-tuple-element.18) | copy-start | bytes 6148
  82.7 2.1 %copy-start.9 = (f32[64]{0:T(128)S(1)}, f32[64]{0:T(128)}, u32[]{:S(2)}) copy-start(f32[64]{0:T(128)} %multiply_power_fusion) | copy-start | bytes 772
  82.7 2.1 %copy-start.10 = (f32[64]{0:T(128)S(1)}, f32[64]{0:T(128)}, u32[]{:S(2)}) copy-start(f32[64]{0:T(128)} %subtract_convert_fusion) | copy-start | bytes 772
  82.7 2.2 %copy-start.12 = (s32[64]{0:T(128)S(1)}, s32[64]{0:T(128)}, u32[]{:S(2)}) copy-start(s32[64]{0:T(128)} %get-tuple-element.5) | copy-start | bytes 772
  86.4 16.9 %copy-start.5 = (bf16[2,5120]{1,0:T(2,128)(2,1)S(1)}, bf16[2,5120]{1,0:T(2,128)(2,1)}, u32[]{:S(2)}) copy-start(bf16[2,5120]{1,0:T(2,128)(2,1)} %param.13) | copy-start | bytes 61444

commit v5 on v4

--- a/solution.py
+++ b/solution.py
@@ -139,13 +139,11 @@
         bank_value.transpose(3, 0, 1, 2).reshape(kv_heads, -1).astype(jnp.float32), per_kv, axis=0
     )
     n_key, n_value, n_latent = key_send.shape[1], value_send.shape[1], latent_send.shape[1]
-    received = lax.all_to_all(
-        jnp.concatenate([key_send, value_send, latent_send, up_send], axis=1),
-        "tp",
-        0,
-        0,
-        tiled=True,
-    )
+    kv_send = jnp.concatenate([key_send, value_send, latent_send, up_send], axis=1)
+    kv_width = kv_send.shape[1]
+    kv_pad = (-kv_width) % (8 * 128)
+    kv_send = jnp.pad(kv_send, ((0, 0), (0, kv_pad))).reshape(tp_width, -1, 128)
+    received = lax.all_to_all(kv_send, "tp", 0, 0, tiled=True).reshape(tp_width, -1)[:, :kv_width]
     key_head = (
         received[:, :n_key]
         .reshape(tp_width, group_tokens, entry_slice)

time: 105 us -> 99.2 us (0.945)
  local copies, waits for them, and re-layouts: 19.2 us -> 15.8 us
  other arithmetic: 7.85 us -> 5.9 us
    all_to_all x2 -> x1, local copies, waits for them, and re-layouts: 2.66 us -> 1.66 us  [shards(): lax.all_to_all(kv_send, 'tp', 0, 0, tiled=True).reshape(tp_width, -1)]
    unnamed x38 -> x42, local copies, waits for them, and re-layouts: 5.79 us -> 6.75 us
  transfers between devices with their start and end apart: 2 -> 2, of which waited for: 1 -> 1; matrix products, arithmetic and copies ran while one was open for 7% -> 6% of each run, Pallas kernels for 0% -> 0%
where the time goes in v5:
time: 99.2 us; the launch traced here: 98.6 us
  blocking collectives  42.3 us (43%)
  starting transfers between devices  20.9 us (21%)
  local copies, waits for them, and re-layouts  15.8 us (16%)
  waiting for transfers between devices  9.97 us (10%)
  other arithmetic  5.9 us (6%)
  matrix products  3.12 us (3%)
    all_gather x1, blocking collectives, shards(): gathered = lax.all_gather(hidden, 'tp', axis=0, tiled=True)  26 us
    all_to_all x1, blocking collectives, shards(): lax.all_to_all(block_terms.reshape(tp_width, tok_rows, block_terms.shape[...  16.4 us
    all_to_all x1, starting transfers between devices, shards(): lax.all_to_all(jnp.tile(bank_piece, (req_width, 1)), 'req', 0, 0, tiled=T...  15.8 us
    all_to_all x1, waiting for transfers between devices, shards(): lax.all_to_all(kv_send, 'tp', 0, 0, tiled=True).reshape(tp_width, -1)  9.97 us
    unnamed x42, local copies, waits for them, and re-layouts  6.75 us
    all_to_all x1, starting transfers between devices, shards(): lax.all_to_all(kv_send, 'tp', 0, 0, tiled=True).reshape(tp_width, -1)  5.14 us
    another operation x1, other arithmetic, shards(): jnp.tile(bank_piece, (req_width, 1))  2.07 us
  transfers between devices with their start and end apart: 2, of which 1 were waited for; matrix products, arithmetic and copies ran while one was open for 6% of the time, Pallas kernels for 0%

profile of v5, /device:TPU:1, one launch (start us, length us, event | category | flops | bytes accessed | tf_op | source)
XLA Modules:
  0.0 98.6 jit_solution(15276528907004660217)
XLA Ops:
  0.0 0.8 copy.100
  0.8 0.8 copy.74
  1.6 0.1 reshape.348
  1.7 0.8 copy.73
  2.5 0.1 reshape.346
  2.6 0.1 maximum_reduce_fusion
  2.7 0.3 tile.2
  3.0 0.5 broadcast.201
  3.5 2.1 %reduce.5 = bf16[16,7680]{1,0:T(8,128)(2,1)S(1)} reduce(bf16[16,1,7680]{2,1,0:T(2,128)(2,1)S(1)} %tile.2, bf16[]{:T(256)} %broadcast.201), dimensions={1}, to_apply=%tile.2.reduce_sub_computation | reduce | bytes 491522 | tf_op jit(solution)/shard_map/tile | solution.py:97
  5.6 0.7 reshape.372
  6.3 15.8 %all-to-all-start = ((bf16[16,2,3840]{2,1,0:T(2,128)(2,1)}), bf16[16,2,3840]{2,1,0:T(2,128)(2,1)}, u32[]{:S(2)}, u32[]{:S(2)}) async-start(bf16[16,2,3840]{2,1,0:T(2,128)(2,1)} %reshape.372), calls=%async_computation | async-start | bytes 491520 | tf_op jit(solution)/shard_map/all_to_all | solution.py:97
  22.2 26.0 %all-gather = bf16[32,2,5120]{2,1,0:T(2,128)(2,1)S(1)} all-gather(bf16[1,2,5120]{2,1,0:T(2,128)(2,1)S(1)} %bitcast.125), channel_id=1, replica_groups=mesh['req'=16,'tp'=32] {'tp'}, dimensions={0}, use_global_device_ids=true | all-gather | bytes 675840 | tf_op jit(solution)/shard_map/all_gather | solution.py:112
  48.1 0.2 reshape.366
  48.3 0.2 multiply_reduce_fusion
  48.5 0.3 copy-done.8
  48.9 0.2 multiply_convert_fusion
  49.1 0.4 copy-done.2
  49.5 0.3 convolution_bitcast_fusion.2
  49.8 0.2 copy.71
  50.0 0.5 copy-done.3
  50.5 0.3 fusion.7
  50.8 0.2 copy.72
  50.9 0.1 broadcast_in_dim.65
  51.1 0.7 reshape_reshape.10
  51.7 0.1 broadcast_in_dim.64
  51.9 0.7 reshape_reshape.9
  52.5 0.1 select_reduce_fusion.3
  52.6 0.7 select_reduce_fusion.1
  53.3 0.6 fusion.50
  53.9 1.1 %reshape.373 = bf16[16,1,7680]{2,1,0:T(2,128)(2,1)S(1)} reshape(bf16[16,2,3840]{2,1,0:T(2,128)(2,1)} %all-to-all-done) | data formatting | bytes 491520
  55.1 0.1 copy.77
  55.2 0.6 copy.78
  55.9 0.2 copy.79
  56.1 0.4 reshape.349
  56.6 0.3 copy.75
  56.9 0.3 fusion
  57.2 0.1 copy.76
  57.3 0.1 reshape.371
  57.5 0.9 copy.94
  58.4 5.1 %all-to-all-start.1 = ((f32[32,32,128]{2,1,0:T(8,128)}), f32[32,32,128]{2,1,0:T(8,128)}, u32[]{:S(2)}, u32[]{:S(2)}) async-start(f32[32,32,128]{2,1,0:T(8,128)} %bitcast.54), calls=%async_computation.1 | async-start | bytes 1048576 | tf_op jit(solution)/shard_map/all_to_all | solution.py:146
  63.6 1.0 convolution_add_fusion.1
  64.6 0.7 reshape_reshape.11
  65.2 10.0 %all-to-all-done.1 = f32[32,32,128]{2,1,0:T(8,128)} async-done(((f32[32,32,128]{2,1,0:T(8,128)}), f32[32,32,128]{2,1,0:T(8,128)}, u32[]{:S(2)}, u32[]{:S(2)}) %all-to-all-start.1) | async-done | bytes 524320 | tf_op jit(solution)/shard_map/all_to_all | solution.py:146
  75.2 1.7 %copy.80 = f32[32,32,128]{0,2,1:T(8,128)S(1)} copy(f32[32,32,128]{2,1,0:T(8,128)} %all-to-all-done.1) | data formatting | bytes 1048576 | tf_op jit(solution)/shard_map/all_to_all | solution.py:146
  76.9 0.3 slice_reduce_fusion
  77.2 0.1 bitcast_convert_fusion
  77.4 0.1 convert_element_type.124
  77.5 0.1 fusion.52
  77.6 0.1 copy.89
  77.7 0.1 copy.82
  77.7 0.1 copy.81
  77.9 0.1 copy.86
  78.1 0.1 copy.92
  78.2 0.1 copy.91
  78.2 1.0 copy.83
  79.2 0.2 fusion.2
  79.4 0.2 fusion.45
  79.6 0.2 fusion.53
  79.9 0.3 fusion.4
  80.3 0.5 convolution_convert_fusion
  80.8 0.2 reshape.359
  81.1 16.4 %all_to_all.19 = bf16[32,2,5120]{2,1,0:T(2,128)(2,1)S(1)} all-to-all(bf16[32,2,5120]{2,1,0:T(2,128)(2,1)S(1)} %reshape.359), channel_id=1, replica_groups=mesh['req'=16,'tp'=32] {'tp'}, dimensions={0} | all-to-all | bytes 1310720 | tf_op jit(solution)/shard_map/all_to_all | solution.py:209
  97.4 0.5 convert_reduce_fusion
  98.0 0.6 add_convert_fusion
  (50 shorter events, 0.5 us)
Async XLA Ops:
  0.0 80.3 %copy-start = (bf16[128,5120]{1,0:T(8,128)(2,1)S(1)}, bf16[128,5120]{1,0:T(8,128)(2,1)}, u32[]{:S(2)}) copy-start(bf16[128,5120]{1,0:T(8,128)(2,1)} %param.18) | copy-start | bytes 3932164
  0.0 22.1 %copy-start.6 = (bf16[2,5120]{1,0:T(2,128)(2,1)S(1)}, bf16[2,5120]{1,0:T(2,128)(2,1)}, u32[]{:S(2)}) copy-start(bf16[2,5120]{1,0:T(2,128)(2,1)} %param.13) | copy-start | bytes 61444
  6.3 47.6 %all-to-all-start = ((bf16[16,2,3840]{2,1,0:T(2,128)(2,1)}), bf16[16,2,3840]{2,1,0:T(2,128)(2,1)}, u32[]{:S(2)}, u32[]{:S(2)}) async-start(bf16[16,2,3840]{2,1,0:T(2,128)(2,1)} %reshape.372), calls=%async_computation | async-start | bytes 491520 | tf_op jit(solution)/shard_map/all_to_all | solution.py:97
  48.1 0.7 copy-start.8
  48.5 1.0 copy-start.2
  48.9 1.1 %copy-start.10 = (f32[4,8]{1,0:T(4,128)S(1)}, f32[4,8]{1,0:T(4,128)}, u32[]{:S(2)}) copy-start(f32[4,8]{1,0:T(4,128)} %param.20) | copy-start | bytes 388
  49.5 1.0 copy-start.3
  51.7 0.8 copy-start.15
  51.7 0.9 copy-start.12
  57.4 6.2 %copy-start.14 = (s32[64]{0:T(128)S(1)}, s32[64]{0:T(128)}, u32[]{:S(2)}) copy-start(s32[64]{0:T(128)} %get-tuple-element.6) | copy-start | bytes 772
  57.4 6.2 %copy-start.1 = (bf16[5120,128]{1,0:T(8,128)(2,1)S(1)}, bf16[5120,128]{1,0:T(8,128)(2,1)}, u32[]{:S(2)}) copy-start(bf16[5120,128]{1,0:T(8,128)(2,1)} %param.15) | copy-start | bytes 3932164
  57.4 6.2 %copy-start.11 = (f32[128]{0:T(128)S(1)}, f32[128]{0:T(128)}, u32[]{:S(2)}) copy-start(f32[128]{0:T(128)} %param.19) | copy-start | bytes 1540
  58.4 16.8 %all-to-all-start.1 = ((f32[32,32,128]{2,1,0:T(8,128)}), f32[32,32,128]{2,1,0:T(8,128)}, u32[]{:S(2)}, u32[]{:S(2)}) async-start(f32[32,32,128]{2,1,0:T(8,128)} %bitcast.54), calls=%async_computation.1 | async-start | bytes 1048576 | tf_op jit(solution)/shard_map/all_to_all | solution.py:146
  77.3 1.9 %copy-start.9 = (bf16[64,16]{0,1:T(8,128)(2,1)S(1)}, bf16[64,16]{0,1:T(8,128)(2,1)}, u32[]{:S(2)}) copy-start(bf16[64,16]{0,1:T(8,128)(2,1)} %get-tuple-element.18) | copy-start | bytes 6148
  77.4 1.9 %copy-start.4 = (bf16[256,128]{1,0:T(8,128)(2,1)S(1)}, bf16[256,128]{1,0:T(8,128)(2,1)}, u32[]{:S(2)}) copy-start(bf16[256,128]{1,0:T(8,128)(2,1)} %reshape_reshape.11) | copy-start | bytes 196612
  77.4 1.9 %copy-start.5 = (f32[64,128]{1,0:T(8,128)S(1)}, f32[64,128]{1,0:T(8,128)}, u32[]{:S(2)}) copy-start(f32[64,128]{1,0:T(8,128)} %convolution_add_fusion.1) | copy-start | bytes 98308
  77.4 2.2 %copy-start.13 = (s32[64]{0:T(128)S(1)}, s32[64]{0:T(128)}, u32[]{:S(2)}) copy-start(s32[64]{0:T(128)} %get-tuple-element.5) | copy-start | bytes 772
  81.0 16.9 %copy-start.7 = (bf16[2,5120]{1,0:T(2,128)(2,1)S(1)}, bf16[2,5120]{1,0:T(2,128)(2,1)}, u32[]{:S(2)}) copy-start(bf16[2,5120]{1,0:T(2,128)(2,1)} %param.13) | copy-start | bytes 61444

commit v6 on v5

--- a/solution.py
+++ b/solution.py
@@ -50,9 +50,24 @@
     )
 
 
-def attend(query_rot, key_rot, value_head, segment):
+def rotate_rows(values_t, offset):
+    width = values_t.shape[0]
+    half_width = width // 2
+    frequency = rope_base ** (-(jnp.arange(half_width, dtype=jnp.float32) * 2.0) / width)
+    angles = offset.astype(jnp.float32)[None, :] * frequency[:, None]
+    cosine = jnp.cos(angles)
+    sines = jnp.sin(angles)
+    lower_half = values_t[:half_width]
+    upper_half = values_t[half_width:]
+    return jnp.concatenate(
+        [lower_half * cosine - upper_half * sines, upper_half * cosine + lower_half * sines],
+        axis=0,
+    )
+
+
+def attend(query_rot, key_rot_t, value_head_t, segment):
     scores = jnp.einsum(
-        "qhd,kd->hqk", query_rot, key_rot, preferred_element_type=jnp.float32
+        "qhd,dk->hqk", query_rot, key_rot_t, preferred_element_type=jnp.float32
     ) * HD ** (-0.5)
     places = jnp.arange(segment.shape[0], dtype=jnp.int32)
     allowed = (segment[:, None] == segment[None, :]) & (places[None, :] <= places[:, None])
@@ -60,7 +75,9 @@
     row_max = jnp.max(scores, axis=-1, keepdims=True)
     weights = jnp.exp(scores - row_max)
     probabilities = (weights / jnp.sum(weights, axis=-1, keepdims=True)).astype(jnp.bfloat16)
-    mixed = jnp.einsum("hqk,kd->qhd", probabilities, value_head, preferred_element_type=jnp.float32)
+    mixed = jnp.einsum(
+        "hqk,dk->qhd", probabilities, value_head_t, preferred_element_type=jnp.float32
+    )
     return mixed.astype(jnp.bfloat16)
 
 
@@ -123,17 +140,17 @@
     latent_part = jnp.sum(jnp.where(adapter_pick[:, :, None], terms, 0.0), axis=1)
 
     key_cols = jnp.einsum(
-        "tm,ehm->the", normalized_input, key_weight, preferred_element_type=jnp.float32
+        "tm,ehm->het", normalized_input, key_weight, preferred_element_type=jnp.float32
     )
     value_cols = (
         jnp.einsum(
-            "tm,ehm->the", normalized_input, value_weight, preferred_element_type=jnp.float32
-        )
-        + jnp.transpose(value_bias_vector)[None, :, :]
+            "tm,ehm->het", normalized_input, value_weight, preferred_element_type=jnp.float32
+        )
+        + jnp.transpose(value_bias_vector)[:, :, None]
     )
     per_kv = tp_width // kv_heads
-    key_send = jnp.repeat(key_cols.transpose(1, 0, 2), per_kv, axis=0).reshape(tp_width, -1)
-    value_send = jnp.repeat(value_cols.transpose(1, 0, 2), per_kv, axis=0).reshape(tp_width, -1)
+    key_send = jnp.repeat(key_cols, per_kv, axis=0).reshape(tp_width, -1)
+    value_send = jnp.repeat(value_cols, per_kv, axis=0).reshape(tp_width, -1)
     latent_send = jnp.broadcast_to(latent_part.reshape(1, -1), (tp_width, latent_part.size))
     up_send = jnp.repeat(
         bank_value.transpose(3, 0, 1, 2).reshape(kv_heads, -1).astype(jnp.float32), per_kv, axis=0
@@ -144,19 +161,8 @@
     kv_pad = (-kv_width) % (8 * 128)
     kv_send = jnp.pad(kv_send, ((0, 0), (0, kv_pad))).reshape(tp_width, -1, 128)
     received = lax.all_to_all(kv_send, "tp", 0, 0, tiled=True).reshape(tp_width, -1)[:, :kv_width]
-    key_head = (
-        received[:, :n_key]
-        .reshape(tp_width, group_tokens, entry_slice)
-        .transpose(1, 0, 2)
-        .reshape(group_tokens, HD)
-        .astype(jnp.bfloat16)
-    )
-    value_base = (
-        received[:, n_key : n_key + n_value]
-        .reshape(tp_width, group_tokens, entry_slice)
-        .transpose(1, 0, 2)
-        .reshape(group_tokens, HD)
-    )
+    key_head_t = received[:, :n_key].reshape(HD, group_tokens).astype(jnp.bfloat16)
+    value_base_t = received[:, n_key : n_key + n_value].reshape(HD, group_tokens)
     latent = (
         jnp.sum(
             received[:, n_key + n_value : n_key + n_value + n_latent].reshape(
@@ -185,22 +191,21 @@
             preferred_element_type=jnp.float32,
         )
     )
-    value_head = (
-        value_base
-        + jnp.dot(
+    value_head_t = (
+        value_base_t
+        + jnp.einsum(
+            "ta,ae->et",
             value_latent,
             value_up_head.astype(jnp.bfloat16).reshape(-1, HD),
             preferred_element_type=jnp.float32,
         )
     ).astype(jnp.bfloat16)
 
-    key_rot = rotate(key_head.astype(jnp.float32).reshape(group_tokens, 1, HD), offset)[
-        :, 0, :
-    ].astype(jnp.bfloat16)
+    key_rot_t = rotate_rows(key_head_t.astype(jnp.float32), offset).astype(jnp.bfloat16)
     query_rot = rotate(query_rows.reshape(group_tokens, head_count, HD), offset).astype(
         jnp.bfloat16
     )
-    mixed_heads = attend(query_rot, key_rot, value_head, segment).reshape(
+    mixed_heads = attend(query_rot, key_rot_t, value_head_t, segment).reshape(
         group_tokens, head_count * HD
     )
     block_terms = jnp.dot(mixed_heads, output_weight, preferred_element_type=jnp.float32).astype(

time: 99.2 us -> 95.8 us (0.966)
  local copies, waits for them, and re-layouts: 15.8 us -> 13 us
    unnamed x42 -> x36, local copies, waits for them, and re-layouts: 6.75 us -> 5.2 us
    another operation x2, local copies, waits for them, and re-layouts: 1.31 us -> 0.21 us  [the longest x1 0.1 us: shards(): key_send = jnp.repeat(key_cols, per_kv, axis=0).reshape(tp_width, -1)]
  transfers between devices with their start and end apart: 2 -> 2, of which waited for: 1 -> 1; matrix products, arithmetic and copies ran while one was open for 6% -> 4% of each run, Pallas kernels for 0% -> 0%
where the time goes in v6:
time: 95.8 us; the launch traced here: 95.2 us
  blocking collectives  42.3 us (44%)
  starting transfers between devices  20.9 us (22%)
  local copies, waits for them, and re-layouts  13 us (14%)
  waiting for transfers between devices  9.99 us (10%)
  other arithmetic  5.42 us (6%)
  matrix products  3.12 us (3%)
    all_gather x1, blocking collectives, shards(): gathered = lax.all_gather(hidden, 'tp', axis=0, tiled=True)  26 us
    all_to_all x1, blocking collectives, shards(): lax.all_to_all(block_terms.reshape(tp_width, tok_rows, block_terms.shape[...  16.4 us
    all_to_all x1, starting transfers between devices, shards(): lax.all_to_all(jnp.tile(bank_piece, (req_width, 1)), 'req', 0, 0, tiled=T...  15.7 us
    all_to_all x1, waiting for transfers between devices, shards(): lax.all_to_all(kv_send, 'tp', 0, 0, tiled=True).reshape(tp_width, -1)  9.99 us
    unnamed x36, local copies, waits for them, and re-layouts  5.2 us
    all_to_all x1, starting transfers between devices, shards(): lax.all_to_all(kv_send, 'tp', 0, 0, tiled=True).reshape(tp_width, -1)  5.13 us
    another operation x1, other arithmetic, shards(): jnp.tile(bank_piece, (req_width, 1))  2.07 us
  transfers between devices with their start and end apart: 2, of which 1 were waited for; matrix products, arithmetic and copies ran while one was open for 4% of the time, Pallas kernels for 0%

profile of v6, /device:TPU:1, one launch (start us, length us, event | category | flops | bytes accessed | tf_op | source)
XLA Modules:
  0.0 95.2 jit_solution(7707406530739789139)
XLA Ops:
  0.0 0.8 copy.90
  0.8 0.8 copy.67
  1.6 0.1 reshape.341
  1.7 0.8 copy.66
  2.5 0.1 reshape.339
  2.6 0.1 maximum_reduce_fusion
  2.7 0.3 tile.2
  3.0 0.5 broadcast.212
  3.5 2.1 %reduce.5 = bf16[16,7680]{1,0:T(8,128)(2,1)S(1)} reduce(bf16[16,1,7680]{2,1,0:T(2,128)(2,1)S(1)} %tile.2, bf16[]{:T(256)} %broadcast.212), dimensions={1}, to_apply=%tile.2.reduce_sub_computation | reduce | bytes 491522 | tf_op jit(solution)/shard_map/tile | solution.py:114
  5.6 0.7 reshape.362
  6.3 15.7 %all-to-all-start = ((bf16[16,2,3840]{2,1,0:T(2,128)(2,1)}), bf16[16,2,3840]{2,1,0:T(2,128)(2,1)S(1)}, u32[]{:S(2)}, u32[]{:S(2)}) async-start(bf16[16,2,3840]{2,1,0:T(2,128)(2,1)} %reshape.362), calls=%async_computation | async-start | bytes 491520 | tf_op jit(solution)/shard_map/all_to_all | solution.py:114
  22.1 26.0 %all-gather = bf16[32,2,5120]{2,1,0:T(2,128)(2,1)S(1)} all-gather(bf16[1,2,5120]{2,1,0:T(2,128)(2,1)S(1)} %bitcast.102), channel_id=1, replica_groups=mesh['req'=16,'tp'=32] {'tp'}, dimensions={0}, use_global_device_ids=true | all-gather | bytes 675840 | tf_op jit(solution)/shard_map/all_gather | solution.py:129
  48.1 0.2 reshape.356
  48.3 0.2 multiply_reduce_fusion
  48.5 0.3 copy-done.8
  48.8 0.2 multiply_convert_fusion
  49.0 0.4 copy-done.2
  49.5 0.3 fusion.7
  49.8 0.0 copy-done.3
  49.8 0.3 convolution_bitcast_fusion.2
  50.1 0.1 reshape_reshape.9
  50.3 0.1 reshape_reshape.10
  50.4 0.1 select_reduce_fusion.3
  50.5 0.6 select_reduce_fusion.1
  51.1 0.2 reshape.363
  51.4 0.1 copy.70
  51.5 0.6 copy.71
  52.2 0.2 copy.72
  52.4 0.4 reshape.342
  52.9 0.3 copy.68
  53.2 0.3 fusion
  53.5 0.1 copy.69
  53.6 0.1 reshape.361
  53.8 0.9 copy.84
  54.7 5.1 %all-to-all-start.1 = ((f32[32,32,128]{2,1,0:T(8,128)}), f32[32,32,128]{2,1,0:T(8,128)}, u32[]{:S(2)}, u32[]{:S(2)}) async-start(f32[32,32,128]{2,1,0:T(8,128)} %bitcast.43), calls=%async_computation.1 | async-start | bytes 1048576 | tf_op jit(solution)/shard_map/all_to_all | solution.py:163
  59.9 1.0 %convolution_add_fusion.1 = f32[64,128]{1,0:T(8,128)} fusion(bf16[64,5120]{1,0:T(8,128)(2,1)S(1)} %multiply_convert_fusion, bf16[5120,128]{1,0:T(8,128)(2,1)S(1)} %copy-done.1, f32[128]{0:T(128)S(1)} %copy-done.10), kind=kOutput, calls=%fused_computation.10 | convolution fusion | flops 83894272 | bytes 1999360 | tf_op jit(solution)/shard_map/dot_general | solution.py:186
  60.9 0.7 reshape_reshape.11
  61.5 10.0 %all-to-all-done.1 = f32[32,32,128]{2,1,0:T(8,128)} async-done(((f32[32,32,128]{2,1,0:T(8,128)}), f32[32,32,128]{2,1,0:T(8,128)}, u32[]{:S(2)}, u32[]{:S(2)}) %all-to-all-start.1) | async-done | bytes 524320 | tf_op jit(solution)/shard_map/all_to_all | solution.py:163
  71.5 1.7 %copy.73 = f32[32,32,128]{0,2,1:T(8,128)S(1)} copy(f32[32,32,128]{2,1,0:T(8,128)} %all-to-all-done.1) | data formatting | bytes 1048576 | tf_op jit(solution)/shard_map/all_to_all | solution.py:163
  73.2 0.3 slice_reduce_fusion
  73.5 0.1 bitcast_convert_fusion
  73.7 0.1 convert_element_type.104
  73.8 0.1 fusion.53
  73.9 0.1 copy.81
  73.9 0.1 copy.76
  74.0 0.1 copy.74
  74.1 0.1 reshape.347
  74.2 0.1 copy.78
  74.3 0.1 fusion.52
  74.4 0.1 copy.80
  74.4 0.1 slice.62
  74.5 0.1 copy.79
  74.6 0.1 slice.60
  74.7 0.9 copy.75
  75.7 0.2 fusion.2
  75.8 0.2 fusion.46
  76.0 0.2 fusion.26
  76.3 0.2 fusion.54
  76.5 0.3 fusion.4
  76.9 0.5 convolution_convert_fusion
  77.4 0.2 reshape.351
  77.7 16.4 %all_to_all.19 = bf16[32,2,5120]{2,1,0:T(2,128)(2,1)S(1)} all-to-all(bf16[32,2,5120]{2,1,0:T(2,128)(2,1)S(1)} %reshape.351), channel_id=1, replica_groups=mesh['req'=16,'tp'=32] {'tp'}, dimensions={0} | all-to-all | bytes 1310720 | tf_op jit(solution)/shard_map/all_to_all | solution.py:214
  94.0 0.5 convert_reduce_fusion
  94.6 0.6 add_convert_fusion
  (49 shorter events, 0.4 us)
Async XLA Ops:
  0.0 76.9 %copy-start = (bf16[128,5120]{1,0:T(8,128)(2,1)S(1)}, bf16[128,5120]{1,0:T(8,128)(2,1)}, u32[]{:S(2)}) copy-start(bf16[128,5120]{1,0:T(8,128)(2,1)} %param.18) | copy-start | bytes 3932164
  0.0 22.1 %copy-start.6 = (bf16[2,5120]{1,0:T(2,128)(2,1)S(1)}, bf16[2,5120]{1,0:T(2,128)(2,1)}, u32[]{:S(2)}) copy-start(bf16[2,5120]{1,0:T(2,128)(2,1)} %param.13) | copy-start | bytes 61444
  6.3 44.8 %all-to-all-start = ((bf16[16,2,3840]{2,1,0:T(2,128)(2,1)}), bf16[16,2,3840]{2,1,0:T(2,128)(2,1)S(1)}, u32[]{:S(2)}, u32[]{:S(2)}) async-start(bf16[16,2,3840]{2,1,0:T(2,128)(2,1)} %reshape.362), calls=%async_computation | async-start | bytes 491520 | tf_op jit(solution)/shard_map/all_to_all | solution.py:114
  48.1 0.7 copy-start.8
  48.5 1.0 %copy-start.2 = (bf16[4,8,5120]{2,1,0:T(8,128)(2,1)S(1)}, bf16[4,8,5120]{2,1,0:T(8,128)(2,1)}, u32[]{:S(2)}) copy-start(bf16[4,8,5120]{2,1,0:T(8,128)(2,1)} %param.17) | copy-start | bytes 983044
  48.5 1.0 %copy-start.9 = (f32[4,8]{1,0:T(4,128)S(1)}, f32[4,8]{1,0:T(4,128)}, u32[]{:S(2)}) copy-start(f32[4,8]{1,0:T(4,128)} %param.20) | copy-start | bytes 388
  48.8 1.0 %copy-start.3 = (bf16[4,8,5120]{2,1,0:T(8,128)(2,1)S(1)}, bf16[4,8,5120]{2,1,0:T(8,128)(2,1)}, u32[]{:S(2)}) copy-start(bf16[4,8,5120]{2,1,0:T(8,128)(2,1)} %param.16) | copy-start | bytes 983044
  49.0 1.4 %copy-start.13 = (s32[1,8]{1,0:T(1,128)S(1)}, s32[1,8]{1,0:T(1,128)}, u32[]{:S(2)}) copy-start(s32[1,8]{1,0:T(1,128)} %param.24) | copy-start | bytes 100
  49.0 1.5 %copy-start.11 = (s32[1,8]{1,0:T(1,128)S(1)}, s32[1,8]{1,0:T(1,128)}, u32[]{:S(2)}) copy-start(s32[1,8]{1,0:T(1,128)} %param.25) | copy-start | bytes 100
  53.7 6.1 %copy-start.1 = (bf16[5120,128]{1,0:T(8,128)(2,1)S(1)}, bf16[5120,128]{1,0:T(8,128)(2,1)}, u32[]{:S(2)}) copy-start(bf16[5120,128]{1,0:T(8,128)(2,1)} %param.15) | copy-start | bytes 3932164
  53.7 6.1 %copy-start.10 = (f32[128]{0:T(128)S(1)}, f32[128]{0:T(128)}, u32[]{:S(2)}) copy-start(f32[128]{0:T(128)} %param.19) | copy-start | bytes 1540
  54.7 16.8 %all-to-all-start.1 = ((f32[32,32,128]{2,1,0:T(8,128)}), f32[32,32,128]{2,1,0:T(8,128)}, u32[]{:S(2)}, u32[]{:S(2)}) async-start(f32[32,32,128]{2,1,0:T(8,128)} %bitcast.43), calls=%async_computation.1 | async-start | bytes 1048576 | tf_op jit(solution)/shard_map/all_to_all | solution.py:163
  73.7 2.0 %copy-start.4 = (bf16[256,128]{1,0:T(8,128)(2,1)S(1)}, bf16[256,128]{1,0:T(8,128)(2,1)}, u32[]{:S(2)}) copy-start(bf16[256,128]{1,0:T(8,128)(2,1)} %reshape_reshape.11) | copy-start | bytes 196612
  73.7 2.0 %copy-start.5 = (f32[64,128]{1,0:T(8,128)S(1)}, f32[64,128]{1,0:T(8,128)}, u32[]{:S(2)}) copy-start(f32[64,128]{1,0:T(8,128)} %convolution_add_fusion.1) | copy-start | bytes 98308
  73.9 2.4 %copy-start.12 = (s32[64]{0:T(128)S(1)}, s32[64]{0:T(128)}, u32[]{:S(2)}) copy-start(s32[64]{0:T(128)} %get-tuple-element.5) | copy-start | bytes 772
  77.7 16.9 %copy-start.7 = (bf16[2,5120]{1,0:T(2,128)(2,1)S(1)}, bf16[2,5120]{1,0:T(2,128)(2,1)}, u32[]{:S(2)}) copy-start(bf16[2,5120]{1,0:T(2,128)(2,1)} %param.13) | copy-start | bytes 61444

commit v7 on v6

--- a/solution.py
+++ b/solution.py
@@ -172,11 +172,8 @@
         )
         .astype(jnp.bfloat16)
     )
-    value_up_head = (
-        received[:, n_key + n_value + n_latent :]
-        .reshape(tp_width, adapter_total, rank_extent, entry_slice)
-        .transpose(1, 2, 0, 3)
-        .reshape(adapter_total, rank_extent, HD)
+    value_up_rows = received[:, n_key + n_value + n_latent :].reshape(
+        tp_width, adapter_total * rank_extent, entry_slice
     )
 
     pick = adapter_pick.astype(jnp.bfloat16)
@@ -194,11 +191,11 @@
     value_head_t = (
         value_base_t
         + jnp.einsum(
-            "ta,ae->et",
+            "ta,sae->set",
             value_latent,
-            value_up_head.astype(jnp.bfloat16).reshape(-1, HD),
+            value_up_rows.astype(jnp.bfloat16),
             preferred_element_type=jnp.float32,
-        )
+        ).reshape(HD, group_tokens)
     ).astype(jnp.bfloat16)
 
     key_rot_t = rotate_rows(key_head_t.astype(jnp.float32), offset).astype(jnp.bfloat16)

time: 95.8 us -> 93.5 us (0.976)
  local copies, waits for them, and re-layouts: 13 us -> 10.3 us
  matrix products: 3.12 us -> 4.66 us
    all_to_all x1 -> x0, local copies, waits for them, and re-layouts: 1.66 us -> none  [shards(): lax.all_to_all(kv_send, 'tp', 0, 0, tiled=True).reshape(tp_width, -1)]
    dot_general x1, matrix products: 0.29 us -> 1.26 us  [shards(): jnp.einsum('tm,ehm->het', normalized_input, key_weight, preferred_element...]
    unnamed x36 -> x26, local copies, waits for them, and re-layouts: 5.2 us -> 5.74 us
  transfers between devices with their start and end apart: 2 -> 2, of which waited for: 1 -> 1; matrix products, arithmetic and copies ran while one was open for 4% -> 5% of each run, Pallas kernels for 0% -> 0%
where the time goes in v7:
time: 93.5 us; the launch traced here: 92.9 us
  blocking collectives  42.3 us (45%)
  starting transfers between devices  20.8 us (22%)
  local copies, waits for them, and re-layouts  10.3 us (11%)
  waiting for transfers between devices  9.85 us (11%)
  matrix products  4.66 us (5%)
  other arithmetic  4.52 us (5%)
    all_gather x1, blocking collectives, shards(): gathered = lax.all_gather(hidden, 'tp', axis=0, tiled=True)  26 us
    all_to_all x1, blocking collectives, shards(): lax.all_to_all(block_terms.reshape(tp_width, tok_rows, block_terms.shape[...  16.4 us
    all_to_all x1, starting transfers between devices, shards(): lax.all_to_all(jnp.tile(bank_piece, (req_width, 1)), 'req', 0, 0, tiled=T...  15.7 us
    all_to_all x1, waiting for transfers between devices, shards(): lax.all_to_all(kv_send, 'tp', 0, 0, tiled=True).reshape(tp_width, -1)  9.85 us
    unnamed x26, local copies, waits for them, and re-layouts  5.74 us
    all_to_all x1, starting transfers between devices, shards(): lax.all_to_all(kv_send, 'tp', 0, 0, tiled=True).reshape(tp_width, -1)  5.08 us
    another operation x1, other arithmetic, shards(): jnp.tile(bank_piece, (req_width, 1))  2.07 us
  transfers between devices with their start and end apart: 2, of which 1 were waited for; matrix products, arithmetic and copies ran while one was open for 5% of the time, Pallas kernels for 0%

profile of v7, /device:TPU:1, one launch (start us, length us, event | category | flops | bytes accessed | tf_op | source)
XLA Modules:
  0.0 92.9 jit_solution(2929217116227379337)
XLA Ops:
  0.0 0.9 %copy.56 = bf16[1,160,32]{2,1,0:T(8,128)(2,1)S(1)} copy(bf16[1,160,32]{1,2,0:T(8,128)(2,1)} %param.21) | data formatting | bytes 20480 | tf_op args[8]
  1.0 0.1 reshape.350
  1.1 0.8 copy.57
  1.8 0.1 reshape.352
  1.9 0.7 copy.79
  2.6 0.1 maximum_reduce_fusion
  2.7 0.3 tile.2
  3.0 0.5 broadcast.220
  3.5 2.1 %reduce.5 = bf16[16,7680]{1,0:T(8,128)(2,1)S(1)} reduce(bf16[16,1,7680]{2,1,0:T(2,128)(2,1)S(1)} %tile.2, bf16[]{:T(256)} %broadcast.220), dimensions={1}, to_apply=%tile.2.reduce_sub_computation | reduce | bytes 491522 | tf_op jit(solution)/shard_map/tile | solution.py:114
  5.6 0.7 reshape.372
  6.3 15.7 %all-to-all-start = ((bf16[16,2,3840]{2,1,0:T(2,128)(2,1)}), bf16[16,2,3840]{2,1,0:T(2,128)(2,1)S(1)}, u32[]{:S(2)}, u32[]{:S(2)}) async-start(bf16[16,2,3840]{2,1,0:T(2,128)(2,1)} %reshape.372), calls=%async_computation | async-start | bytes 491520 | tf_op jit(solution)/shard_map/all_to_all | solution.py:114
  22.1 26.0 %all-gather = bf16[32,2,5120]{2,1,0:T(2,128)(2,1)S(1)} all-gather(bf16[1,2,5120]{2,1,0:T(2,128)(2,1)S(1)} %bitcast.107), channel_id=1, replica_groups=mesh['req'=16,'tp'=32] {'tp'}, dimensions={0}, use_global_device_ids=true | all-gather | bytes 675840 | tf_op jit(solution)/shard_map/all_gather | solution.py:129
  48.1 0.2 reshape.367
  48.3 0.0 copy-start.3
  48.3 0.2 multiply_reduce_fusion
  48.5 0.0 copy-start.4
  48.5 0.5 copy-done.3
  49.0 0.2 multiply_convert_fusion
  49.2 0.0 copy-start.7
  49.2 0.0 copy-start.6
  49.2 0.2 copy-done.1
  49.5 0.3 fusion.6
  49.8 0.1 reshape_reshape.10
  49.9 1.3 %convolution_bitcast_fusion.1 = f32[8,4,64]{2,0,1:T(8,128)S(1)} fusion(bf16[4,8,5120]{2,1,0:T(8,128)(2,1)} %param.16, bf16[64,5120]{1,0:T(8,128)(2,1)S(1)} %multiply_convert_fusion), kind=kOutput, calls=%fused_computation.18 | convolution fusion | flops 20971520 | bytes 991232 | tf_op jit(solution)/shard_map/tm,ehm->het/dot_general | solution.py:142
  51.2 0.1 reshape_reshape.9
  51.3 0.1 select_reduce_fusion.3
  51.4 0.1 select_reduce_fusion.1
  51.5 0.0 all-to-all-done
  51.5 0.2 reshape.373
  51.9 0.4 reshape.353
  52.3 0.3 copy.58
  52.6 0.3 fusion
  52.9 0.1 copy.59
  53.0 0.1 reshape.371
  53.1 0.1 copy.60
  53.2 0.6 copy.61
  53.8 0.2 copy.62
  54.2 0.0 copy-start.5
  54.2 0.9 copy.70
  55.1 5.1 %all-to-all-start.1 = ((f32[32,32,128]{2,1,0:T(8,128)}), f32[32,32,128]{2,1,0:T(8,128)S(1)}, u32[]{:S(2)}, u32[]{:S(2)}) async-start(f32[32,32,128]{2,1,0:T(8,128)} %bitcast.41), calls=%async_computation.1 | async-start | bytes 1048576 | tf_op jit(solution)/shard_map/all_to_all | solution.py:163
  60.2 1.7 %convolution_add_fusion.1 = f32[64,128]{1,0:T(8,128)S(1)} fusion(bf16[64,5120]{1,0:T(8,128)(2,1)S(1)} %multiply_convert_fusion, bf16[5120,128]{1,0:T(8,128)(2,1)} %param.15, f32[128]{0:T(128)S(1)} %copy-done.5), kind=kOutput, calls=%fused_computation.10 | convolution fusion | flops 83894272 | bytes 1999360 | tf_op jit(solution)/shard_map/dot_general | solution.py:183
  62.0 9.8 %all-to-all-done.1 = f32[32,32,128]{2,1,0:T(8,128)S(1)} async-done(((f32[32,32,128]{2,1,0:T(8,128)}), f32[32,32,128]{2,1,0:T(8,128)S(1)}, u32[]{:S(2)}, u32[]{:S(2)}) %all-to-all-start.1) | async-done | bytes 524320 | tf_op jit(solution)/shard_map/all_to_all | solution.py:163
  71.8 0.3 copy.77
  72.1 0.3 copy.80
  72.5 0.1 convert_element_type.96
  72.6 0.1 fusion.49
  72.7 0.1 copy.65
  72.8 0.1 copy.67
  72.8 0.1 slice.60
  72.9 0.1 slice.62
  73.0 0.2 copy.63
  73.2 0.2 copy.64
  73.4 0.1 reshape.358
  73.5 0.1 copy.66
  73.6 0.2 fusion.2
  73.7 0.2 fusion.41
  73.9 0.2 fusion.23
  74.2 0.2 fusion.50
  74.4 0.2 fusion.3
  74.6 0.5 convolution_convert_fusion
  75.2 0.2 reshape.362
  75.4 16.4 %all_to_all.19 = bf16[32,2,5120]{2,1,0:T(2,128)(2,1)S(1)} all-to-all(bf16[32,2,5120]{2,1,0:T(2,128)(2,1)S(1)} %reshape.362), channel_id=1, replica_groups=mesh['req'=16,'tp'=32] {'tp'}, dimensions={0} | all-to-all | bytes 1310720 | tf_op jit(solution)/shard_map/all_to_all | solution.py:211
  91.8 0.5 convert_reduce_fusion
  92.3 0.6 add_convert_fusion
  (36 shorter events, 0.5 us)
Async XLA Ops:
  0.0 74.6 %copy-start = (bf16[128,5120]{1,0:T(8,128)(2,1)S(1)}, bf16[128,5120]{1,0:T(8,128)(2,1)}, u32[]{:S(2)}) copy-start(bf16[128,5120]{1,0:T(8,128)(2,1)} %param.18) | copy-start | bytes 3932164
  0.0 22.1 %copy-start.2 = (bf16[2,5120]{1,0:T(2,128)(2,1)S(1)}, bf16[2,5120]{1,0:T(2,128)(2,1)}, u32[]{:S(2)}) copy-start(bf16[2,5120]{1,0:T(2,128)(2,1)} %param.13) | copy-start | bytes 61444
  6.3 45.2 %all-to-all-start = ((bf16[16,2,3840]{2,1,0:T(2,128)(2,1)}), bf16[16,2,3840]{2,1,0:T(2,128)(2,1)S(1)}, u32[]{:S(2)}, u32[]{:S(2)}) async-start(bf16[16,2,3840]{2,1,0:T(2,128)(2,1)} %reshape.372), calls=%async_computation | async-start | bytes 491520 | tf_op jit(solution)/shard_map/all_to_all | solution.py:114
  48.3 0.7 copy-start.3
  48.5 1.0 %copy-start.1 = (bf16[4,8,5120]{2,1,0:T(8,128)(2,1)S(1)}, bf16[4,8,5120]{2,1,0:T(8,128)(2,1)}, u32[]{:S(2)}) copy-start(bf16[4,8,5120]{2,1,0:T(8,128)(2,1)} %param.17) | copy-start | bytes 983044
  48.5 1.0 %copy-start.4 = (f32[4,8]{1,0:T(4,128)S(1)}, f32[4,8]{1,0:T(4,128)}, u32[]{:S(2)}) copy-start(f32[4,8]{1,0:T(4,128)} %param.20) | copy-start | bytes 388
  49.2 2.1 %copy-start.7 = (s32[1,8]{1,0:T(1,128)S(1)}, s32[1,8]{1,0:T(1,128)}, u32[]{:S(2)}) copy-start(s32[1,8]{1,0:T(1,128)} %param.24) | copy-start | bytes 100
  49.2 2.2 %copy-start.6 = (s32[1,8]{1,0:T(1,128)S(1)}, s32[1,8]{1,0:T(1,128)}, u32[]{:S(2)}) copy-start(s32[1,8]{1,0:T(1,128)} %param.25) | copy-start | bytes 100
  54.2 6.1 %copy-start.5 = (f32[128]{0:T(128)S(1)}, f32[128]{0:T(128)}, u32[]{:S(2)}) copy-start(f32[128]{0:T(128)} %param.19) | copy-start | bytes 1540
  55.1 16.7 %all-to-all-start.1 = ((f32[32,32,128]{2,1,0:T(8,128)}), f32[32,32,128]{2,1,0:T(8,128)S(1)}, u32[]{:S(2)}, u32[]{:S(2)}) async-start(f32[32,32,128]{2,1,0:T(8,128)} %bitcast.41), calls=%async_computation.1 | async-start | bytes 1048576 | tf_op jit(solution)/shard_map/all_to_all | solution.py:163
